TPU v7x, 32 devices: a whole 2x2x4 slice. The times are simulated.
32 devices in a mesh: grp: 4 (over z), exp: 8 (over y, x, core).
Axes of the slice: x: 2, y: 2, z: 4, core: 2. Of those that a mesh axis runs over, the one named last changes fastest.
Arguments:
- cotangent: bfloat16 [4096, 1440], P(('grp', 'exp')), may hold values from -6 to 6
- hidden: bfloat16 [4096, 4, 1440], P(('grp', 'exp')), may hold values from -0.29882812 to 0.29882812
- gates: bfloat16 [4096, 4], P(('grp', 'exp')), may hold values from 0.049804688 to 1
- expert_ids: int32 [4096, 4], P(('grp', 'exp')), may hold values from 0 to 15, all different within a row; in each aligned block of 128 rows (0 to 127, 128 to 255, ...) at most 40 rows name the same one
- group_counts: int32 [4], P('grp'), may hold values from 146 to 1024, as said below
- w_down: bfloat16 [16, 1440, 1440], P('exp', 'grp'), may hold values from -0.15625 to 0.15625
Outputs:
- d_hidden: bfloat16 [4096, 4, 1440], P(('grp', 'exp'))
- d_gate: bfloat16 [4096, 4], P(('grp', 'exp'))
- d_weight: float32 [16, 1440, 1440], P('exp', 'grp')
Inputs may be any that keep to these rules, and one draw needn't show every extreme that they name: `expert_ids`: within the rows of one device no expert is named more than 40 times, and every expert is named somewhere. `group_counts`: some group has all 1024 slots live, and some group only 146.
All inputs are finite; a program needn't handle non-finite values.
Results may differ from a plain program's by a relative error of at most 0.015.
Values may be sent and summed in bfloat16 or wider, within the bound.
No kernel may reach another device: no remote copies, remote signals or barrier semaphores. Data moves between devices by JAX's collectives and lax.ppermute only.
A program may use at most 128 MiB of HBM per device.

v0:
```python
import jax
import jax.numpy as jnp
from jax import lax
from jax.sharding import PartitionSpec as P

LOSS_SCALE = 32768


def dispatch(ids, wt, cot, hid, experts, exp_dev, most, n_exp):
    n, per = ids.shape
    top = per * n // cot.shape[0]
    rows = n_exp * n * exp_dev * most
    onehot = (ids[:, :, None] == jnp.arange(experts, dtype=jnp.int32)).astype(jnp.int32)
    rank = jnp.sum((jnp.cumsum(onehot, axis=1) - onehot) * onehot, axis=2)
    src = jnp.arange(n, dtype=jnp.int32)[:, None]
    target = ((((ids // exp_dev) * n + src) * exp_dev + ids % exp_dev) * most + rank).reshape(-1)
    pick = (target[None, :] == jnp.arange(rows, dtype=jnp.int32)[:, None]).astype(jnp.bfloat16)
    pick_tok = jnp.sum(pick.reshape(rows, n * per // top, top), axis=2)
    per_dest = n * exp_dev * most
    dy_buf = jnp.dot(pick_tok, cot, preferred_element_type=jnp.float32).astype(jnp.bfloat16)
    gate_buf = jnp.dot(pick, wt, preferred_element_type=jnp.float32).astype(jnp.bfloat16)
    dy_r = lax.all_to_all(dy_buf.reshape(n_exp, per_dest, -1), "exp", 0, 0, tiled=True)
    gate_r = lax.all_to_all(gate_buf.reshape(n_exp, per_dest), "exp", 0, 0, tiled=True)
    hid_r = None
    if hid is not None:
        hid_buf = jnp.dot(pick, hid, preferred_element_type=jnp.float32).astype(jnp.bfloat16)
        hid_r = lax.all_to_all(hid_buf.reshape(n_exp, per_dest, -1), "exp", 0, 0, tiled=True)
    return pick, dy_r, gate_r, hid_r


def proj_home(pick, dy_r, w_down, n, most):
    n_exp, exp_dev = dy_r.shape[0], w_down.shape[0]
    dy_r = dy_r.reshape(n_exp, n, exp_dev, most, -1)
    proj = jnp.einsum("cgjmd,jfd->cgjmf", dy_r, w_down, preferred_element_type=jnp.float32)
    back = lax.all_to_all(
        proj.astype(jnp.bfloat16).reshape(n_exp, n * exp_dev * most, -1), "exp", 0, 0, tiled=True
    )
    return jnp.dot(pick.T, back.reshape(-1, back.shape[-1]), preferred_element_type=jnp.float32)


def body(cotangent, hidden, gates, expert_ids, group_counts, w_down):
    tok, top = expert_ids.shape
    ffw = hidden.shape[2]
    width = cotangent.shape[1]
    n_exp = lax.axis_size("exp")
    n_grp = lax.axis_size("grp")
    exp_dev, f_loc = w_down.shape[0], w_down.shape[1]
    experts = exp_dev * n_exp
    most = 5 * tok * top // (4 * experts)
    me = lax.axis_index("grp")

    count = group_counts[0]
    first_row = lax.axis_index("exp") * tok
    live = (first_row + jnp.arange(tok, dtype=jnp.int32) < count).astype(jnp.float32)
    weighted = (gates.astype(jnp.float32) * live[:, None]).astype(jnp.bfloat16)

    digits = jnp.stack([count // 64, count % 64]).astype(jnp.bfloat16)
    packed = jnp.concatenate(
        [cotangent, expert_ids.astype(jnp.bfloat16), weighted, jnp.broadcast_to(digits, (tok, 2))], axis=1
    )
    got = lax.all_gather(packed, "grp")
    dig = got[:, 0, width + 2 * top :].astype(jnp.float32)
    total = jnp.sum(dig[:, 0] * 64.0 + dig[:, 1])
    scale = LOSS_SCALE / total

    pick_a, dy_a, gate_a, hid_a = dispatch(
        expert_ids.reshape(1, tok * top), weighted.reshape(-1), cotangent,
        hidden.reshape(tok * top, ffw), experts, exp_dev, most, n_exp,
    )
    gate_fa = gate_a.reshape(n_exp, exp_dev, most).astype(jnp.float32)
    dy_fa = dy_a.reshape(n_exp, exp_dev, most, width)
    scaled = (gate_fa[..., None] * dy_fa.astype(jnp.float32)).astype(jnp.bfloat16)
    partial_grad = (
        jnp.einsum(
            "sjmgf,sjmd->gjfd",
            hid_a.reshape(n_exp, exp_dev, most, n_grp, f_loc),
            scaled,
            preferred_element_type=jnp.float32,
        )
        * scale
    )
    grad_rows = partial_grad.astype(jnp.bfloat16).reshape(n_grp * exp_dev * f_loc, width)
    d_weight = (
        lax.psum_scatter(grad_rows, "grp", scatter_dimension=0, tiled=True)
        .reshape(exp_dev, f_loc, width)
        .astype(jnp.float32)
    )

    rel = (me + jnp.arange(1, n_grp, dtype=jnp.int32)) % n_grp
    got_b = jnp.take(got, rel, axis=0)
    n_b = n_grp - 1
    pick_b, dy_b, _, _ = dispatch(
        got_b[:, :, width : width + top].astype(jnp.int32).reshape(n_b, tok * top),
        got_b[:, :, width + top : width + 2 * top].reshape(-1),
        got_b[:, :, :width].reshape(n_b * tok, width),
        None, experts, exp_dev, most, n_exp,
    )

    proj_rel = jnp.concatenate(
        [proj_home(pick_a, dy_a, w_down, 1, most), proj_home(pick_b, dy_b, w_down, n_b, most)]
    ).astype(jnp.bfloat16).reshape(n_grp, tok, top, f_loc)
    back = (jnp.arange(n_grp, dtype=jnp.int32) - me) % n_grp
    proj_slot = jnp.take(proj_rel, back, axis=0)
    proj_got = lax.all_to_all(proj_slot, "grp", split_axis=0, concat_axis=0, tiled=True)
    proj = jnp.transpose(proj_got, (1, 2, 0, 3)).reshape(tok, top, ffw).astype(jnp.float32)

    d_hidden = (weighted.astype(jnp.float32)[..., None] * proj).astype(jnp.bfloat16)
    inner = jnp.sum(hidden.astype(jnp.float32) * proj, axis=2).astype(jnp.bfloat16)
    d_gate = (inner.astype(jnp.float32) * live[:, None]).astype(jnp.bfloat16)
    return (d_hidden, d_gate, d_weight)


def solution(mesh):
    in_specs = (
        P(("grp", "exp"), None),
        P(("grp", "exp"), None, None),
        P(("grp", "exp"), None),
        P(("grp", "exp"), None),
        P("grp"),
        P("exp", "grp", None),
    )
    out_specs = (P(("grp", "exp"), None, None), P(("grp", "exp"), None), P("exp", "grp", None))
    return jax.shard_map(body, mesh=mesh, in_specs=in_specs, out_specs=out_specs, check_vma=False)
```

profile of v0, /device:TPU:2, one launch (start us, length us, event | category | flops | bytes accessed | tf_op | source)
XLA Modules:
  0.0 332.6 jit_solution(14348242018352758282)
XLA Ops:
  7.2 0.9 copy.162
  8.3 1.2 reduce-window.14
  9.4 0.2 slice_reduce_fusion.1
  10.3 0.7 fusion.91
  11.6 0.3 fusion.42
  12.0 0.7 all_to_all.32
  12.6 4.3 %all-to-all-start.5 = ((bf16[8,1,80]{2,1,0:T(2,128)(2,1)}), bf16[8,1,80]{2,1,0:T(2,128)(2,1)S(1)}, u32[]{:S(2)}, u32[]{:S(2)}) async-start(bf16[8,1,80]{2,1,0:T(2,128)(2,1)} %all_to_all.32), calls=%async_computation.5 | async-start | bytes 8192 | tf_op jit(solution)/shard_map/all_to_all | solution.py:23
  16.9 3.8 %copy.195 = bf16[128,4,1440]{2,1,0:T(4,128)(2,1)} copy(bf16[128,4,1440]{0,2,1:T(8,128)(2,1)} %param.7) | data formatting | bytes 2949120 | tf_op args[1]
  20.7 3.7 %reshape.541 = bf16[512,1440]{1,0:T(8,128)(2,1)} reshape(bf16[128,4,1440]{2,1,0:T(4,128)(2,1)} %copy.195) | data formatting | bytes 2949120 | tf_op jit(solution)/shard_map/reshape | solution.py:68
  24.4 4.0 %convolution_convert_fusion.2 = bf16[640,1440]{0,1:T(8,128)(2,1)} fusion(bf16[512,1440]{1,0:T(8,128)(2,1)} %reshape.541, s32[512]{0:T(512)S(1)} %fusion.82), kind=kOutput, calls=%fused_computation.16 | convolution fusion | flops 944967680 | bytes 3319808 | tf_op jit(solution)/shard_map/dot_general | solution.py:26
  28.5 3.9 %copy.196 = bf16[640,1440]{1,0:T(8,128)(2,1)} copy(bf16[640,1440]{0,1:T(8,128)(2,1)} %convolution_convert_fusion.2) | data formatting | bytes 3686400 | tf_op jit(solution)/shard_map/convert_element_type | solution.py:26
  32.3 4.4 %all-to-all-start.6 = ((bf16[8,80,1440]{2,1,0:T(8,128)(2,1)}), bf16[8,80,1440]{2,1,0:T(8,128)(2,1)}, u32[]{:S(2)}, u32[]{:S(2)}) async-start(bf16[8,80,1440]{2,1,0:T(8,128)(2,1)} %bitcast.136), calls=%async_computation.6 | async-start | bytes 3932160 | tf_op jit(solution)/shard_map/all_to_all | solution.py:27
  37.1 2.5 concatenate.7
  40.2 1.9 convolution_convert_fusion.1
  42.1 3.8 %copy.174 = bf16[640,1440]{1,0:T(8,128)(2,1)} copy(bf16[640,1440]{0,1:T(8,128)(2,1)} %convolution_convert_fusion.1) | data formatting | bytes 3686400 | tf_op jit(solution)/shard_map/convert_element_type | solution.py:20
  46.0 14.6 %all-to-all-done.6 = bf16[8,80,1440]{2,1,0:T(8,128)(2,1)} async-done(((bf16[8,80,1440]{2,1,0:T(8,128)(2,1)}), bf16[8,80,1440]{2,1,0:T(8,128)(2,1)}, u32[]{:S(2)}, u32[]{:S(2)}) %all-to-all-start.6) | async-done | bytes 1843232 | tf_op jit(solution)/shard_map/all_to_all | solution.py:27
  60.6 5.7 %all-to-all-start = ((bf16[8,80,1440]{2,1,0:T(8,128)(2,1)}), bf16[8,80,1440]{2,1,0:T(8,128)(2,1)}, u32[]{:S(2)}, u32[]{:S(2)}) async-start(bf16[8,80,1440]{2,1,0:T(8,128)(2,1)} %bitcast.137), calls=%async_computation | async-start | bytes 3932160 | tf_op jit(solution)/shard_map/all_to_all | solution.py:22
  66.4 5.4 %reshape.543 = bf16[8,2,40,4,360]{4,3,2,1,0:T(4,128)(2,1)} reshape(bf16[8,80,1440]{2,1,0:T(8,128)(2,1)} %all-to-all-done.6) | data formatting | bytes 3686400 | tf_op jit(solution)/shard_map/reshape | solution.py:76
  71.8 5.6 %all-gather.3.cloned.1.call-done = bf16[512,1450]{0,1:T(8,128)(2,1)} async-done(((bf16[128,1450]{0,1:T(8,128)(2,1)}), bf16[512,1450]{0,1:T(8,128)(2,1)}) %all-gather.3.cloned.1.call-update) | async-done | bytes 1484816 | tf_op jit(solution)/shard_map/all_gather | solution.py:61
  77.4 2.6 copy.177
  80.0 0.8 slice.45
  80.9 0.6 add_reduce_fusion
  82.1 8.0 %all-to-all-done = bf16[8,80,1440]{2,1,0:T(8,128)(2,1)} async-done(((bf16[8,80,1440]{2,1,0:T(8,128)(2,1)}), bf16[8,80,1440]{2,1,0:T(8,128)(2,1)}, u32[]{:S(2)}, u32[]{:S(2)}) %all-to-all-start) | async-done | bytes 1843232 | tf_op jit(solution)/shard_map/all_to_all | solution.py:22
  90.1 10.5 %fusion.3 = bf16[4,2,360,1440]{3,2,0,1:T(8,128)(2,1)} fusion(f32[]{:T(128)S(6)} %div.58, bf16[8,2,40,4,360]{4,3,2,1,0:T(4,128)(2,1)} %reshape.543, bf16[8,2,40,1440]{3,2,1,0:T(8,128)(2,1)} %bitcast.8, f32[8,2,40]{2,1,0:T(2,128)S(1)} %reshape.546), kind=kOutput, calls=%fused_computation.8 | convolution fusion | flops 2665267200 | bytes 11983364 | tf_op jit(solution)/shard_map/sjmgf,sjmd->gjfd/dot_general | solution.py:74
  100.6 7.8 %copy.200 = bf16[4,2,360,1440]{3,2,1,0:T(8,128)(2,1)} copy(bf16[4,2,360,1440]{3,2,0,1:T(8,128)(2,1)} %fusion.3) | data formatting | bytes 16588800 | tf_op jit(solution)/shard_map/convert_element_type | solution.py:82
  108.5 0.2 add.249
  108.8 2.6 copy.178
  111.4 2.1 gather_fusion
  113.6 0.2 broadcast_select_fusion.1
  113.7 1.0 copy-done.2
  115.2 0.7 fusion.50
  115.8 7.3 %reduce-window.16 = s32[3,16,4,128]{3,1,2,0:T(8,128)} reduce-window(s32[3,16,4,128]{3,1,2,0:T(8,128)} %fusion.50, s32[]{:T(128)} %constant.137.clone.1), window={size=1x1x1x128 pad=0_0x0_0x0_0x127_0}, to_apply=%region_4.5 | reduce-window | flops 3121152 | bytes 196612 | tf_op jit(solution)/shard_map/reduce-window.2
  123.1 1.3 slice_reduce_fusion
  124.4 1.0 fusion.49
  125.4 0.9 reduce_sum.71
  126.3 1.0 copy.184
  127.3 1.7 copy.185
  129.0 0.7 fusion.75
  129.7 1.9 fusion.4
  131.6 6.6 %convolution_convert_fusion = bf16[1920,1440]{0,1:T(8,128)(2,1)} fusion(bf16[1920,384]{1,0:T(8,128)(2,1)S(1)} %fusion.4, bf16[384,1440]{1,0:T(8,128)(2,1)} %bitcast.142), kind=kOutput, calls=%fused_computation.9 | convolution fusion | flops 2126131200 | bytes 8110080 | tf_op jit(solution)/shard_map/dot_general | solution.py:20
  138.3 8.3 %copy.205 = bf16[1920,1440]{1,0:T(8,128)(2,1)} copy(bf16[1920,1440]{0,1:T(8,128)(2,1)} %convolution_convert_fusion) | data formatting | bytes 11059200 | tf_op jit(solution)/shard_map/reshape | solution.py:22
  146.5 6.2 %all-to-all-start.2 = ((bf16[8,240,1440]{2,1,0:T(8,128)(2,1)}), bf16[8,240,1440]{2,1,0:T(8,128)(2,1)}, u32[]{:S(2)}, u32[]{:S(2)}) async-start(bf16[8,240,1440]{2,1,0:T(8,128)(2,1)} %bitcast.135), calls=%async_computation.2 | async-start | bytes 11796480 | tf_op jit(solution)/shard_map/all_to_all | solution.py:22
  152.7 2.7 fusion.37
  155.4 0.8 copy.176
  156.3 62.4 %all-to-all-done.2 = bf16[8,240,1440]{2,1,0:T(8,128)(2,1)} async-done(((bf16[8,240,1440]{2,1,0:T(8,128)(2,1)}), bf16[8,240,1440]{2,1,0:T(8,128)(2,1)}, u32[]{:S(2)}, u32[]{:S(2)}) %all-to-all-start.2) | async-done | bytes 5529632 | tf_op jit(solution)/shard_map/all_to_all | solution.py:22
  218.7 4.9 %all-to-all-start.1 = ((bf16[8,80,360]{2,1,0:T(8,128)(2,1)}), bf16[8,80,360]{2,1,0:T(8,128)(2,1)S(1)}, u32[]{:S(2)}, u32[]{:S(2)}) async-start(bf16[8,80,360]{2,1,0:T(8,128)(2,1)} %bitcast.14), calls=%async_computation.1 | async-start | bytes 983040 | tf_op jit(solution)/shard_map/all_to_all | solution.py:35
  223.6 5.9 %fusion.23 = bf16[8,3,2,40,360]{4,3,1,0,2:T(8,128)(2,1)S(1)} fusion(bf16[2,360,1440]{2,1,0:T(8,128)(2,1)S(1)} %copy-done, bf16[8,3,2,40,1440]{4,3,2,1,0:T(8,128)(2,1)} %bitcast.24), kind=kOutput, calls=%fused_computation.32 | convolution fusion | flops 1991347200 | bytes 8985600 | tf_op jit(solution)/shard_map/cgjmd,jfd->cgjmf/dot_general | solution.py:34
  229.5 1.3 copy.188
  230.8 0.8 all-to-all-done.1
  231.6 5.7 %all-to-all-start.3 = ((bf16[8,240,360]{2,1,0:T(8,128)(2,1)}), bf16[8,240,360]{2,1,0:T(8,128)(2,1)}, u32[]{:S(2)}, u32[]{:S(2)}) async-start(bf16[8,240,360]{2,1,0:T(8,128)(2,1)} %bitcast.140), calls=%async_computation.3 | async-start | bytes 2949120 | tf_op jit(solution)/shard_map/all_to_all | solution.py:35
  237.3 0.5 fusion.36
  238.0 17.8 %all-to-all-done.3 = bf16[8,240,360]{2,1,0:T(8,128)(2,1)} async-done(((bf16[8,240,360]{2,1,0:T(8,128)(2,1)}), bf16[8,240,360]{2,1,0:T(8,128)(2,1)}, u32[]{:S(2)}, u32[]{:S(2)}) %all-to-all-start.3) | async-done | bytes 1382432 | tf_op jit(solution)/shard_map/all_to_all | solution.py:35
  255.8 4.1 %fusion.10 = bf16[1536,360]{0,1:T(8,128)(2,1)S(1)} fusion(bf16[1920,360]{1,0:T(8,128)(2,1)} %bitcast.29, s32[1536]{0:T(1024)S(1)} %fusion.65), kind=kOutput, calls=%fused_computation.21 | convolution fusion | flops 2126868480 | bytes 2494464 | tf_op jit(solution)/shard_map/dot_general | solution.py:38
  259.9 1.3 pad_maximum_fusion
  261.2 2.6 copy.189
  263.8 3.9 %convert_element_type.165 = bf16[4,128,4,360]{3,2,1,0:T(4,128)(2,1)} reshape(bf16[2048,360]{1,0:T(8,128)(2,1)} %copy.189) | data formatting | bytes 2949120 | tf_op jit(solution)/shard_map/convert_element_type | solution.py:101
  267.6 2.8 copy.190
  270.4 3.3 gather_fusion.1
  273.8 2.8 broadcast_select_fusion
  276.6 2.6 copy.191
  279.1 40.1 %all_to_all.40 = bf16[4,128,4,360]{1,3,2,0:T(8,128)(2,1)S(1)} all-to-all(bf16[4,128,4,360]{1,3,2,0:T(8,128)(2,1)} %copy.191), channel_id=1, replica_groups=mesh['grp'=4,'exp'=8] {'grp'}, dimensions={0} | all-to-all | bytes 2949120 | tf_op jit(solution)/shard_map/all_to_all | solution.py:104
  319.2 1.7 fusion.9
  320.9 0.6 multiply_convert_fusion.1
  321.5 4.3 %convert.26 = f32[2,360,1440]{2,1,0:T(8,128)} convert(bf16[2,360,1440]{2,1,0:T(8,128)(2,1)} %bitcast.141) | non-fusion elementwise | flops 1036800 | bytes 6220800 | tf_op jit(solution)/shard_map/convert_element_type | solution.py:86
  (70 shorter events, 2.6 us)
Async XLA Ops:
  7.2 145.6 %copy-start = (bf16[2,360,1440]{2,1,0:T(8,128)(2,1)S(1)}, bf16[2,360,1440]{2,1,0:T(8,128)(2,1)}, u32[]{:S(2)}) copy-start(bf16[2,360,1440]{2,1,0:T(8,128)(2,1)} %param.11) | copy-start | bytes 6220804
  10.3 0.7 copy-start.7
  11.6 12.8 %copy-start.5 = (s32[512]{0:T(512)}, s32[512]{0:T(512)S(1)}, u32[]{:S(2)}) copy-start(s32[512]{0:T(512)S(1)} %fusion.82) | copy-start | bytes 6148
  12.6 19.7 %all-to-all-start.5 = ((bf16[8,1,80]{2,1,0:T(2,128)(2,1)}), bf16[8,1,80]{2,1,0:T(2,128)(2,1)S(1)}, u32[]{:S(2)}, u32[]{:S(2)}) async-start(bf16[8,1,80]{2,1,0:T(2,128)(2,1)} %all_to_all.32), calls=%async_computation.5 | async-start | bytes 8192 | tf_op jit(solution)/shard_map/all_to_all | solution.py:23
  32.3 4.5 %copy-start.4 = (s32[128,4]{0,1:T(4,128)S(1)}, s32[128,4]{0,1:T(4,128)}, u32[]{:S(2)}) copy-start(s32[128,4]{0,1:T(4,128)} %param.9) | copy-start | bytes 6148
  32.3 4.7 %copy-start.3 = (bf16[128,1440]{0,1:T(8,128)(2,1)S(1)}, bf16[128,1440]{0,1:T(8,128)(2,1)}, u32[]{:S(2)}) copy-start(bf16[128,1440]{0,1:T(8,128)(2,1)} %param.6) | copy-start | bytes 1105924
  32.3 28.2 %all-to-all-start.6 = ((bf16[8,80,1440]{2,1,0:T(8,128)(2,1)}), bf16[8,80,1440]{2,1,0:T(8,128)(2,1)}, u32[]{:S(2)}, u32[]{:S(2)}) async-start(bf16[8,80,1440]{2,1,0:T(8,128)(2,1)} %bitcast.136), calls=%async_computation.6 | async-start | bytes 3932160 | tf_op jit(solution)/shard_map/all_to_all | solution.py:27
  36.8 40.6 %all-gather.3.cloned.1.call-start = ((), (), s32[]{:S(2)}) async-start(), calls=%async_computation.9 | async-start | bytes 1863680 | tf_op jit(solution)/shard_map/all_gather | solution.py:61
  60.6 29.6 %all-to-all-start = ((bf16[8,80,1440]{2,1,0:T(8,128)(2,1)}), bf16[8,80,1440]{2,1,0:T(8,128)(2,1)}, u32[]{:S(2)}, u32[]{:S(2)}) async-start(bf16[8,80,1440]{2,1,0:T(8,128)(2,1)} %bitcast.137), calls=%async_computation | async-start | bytes 3932160 | tf_op jit(solution)/shard_map/all_to_all | solution.py:22
  66.3 255.2 %reduce-scatter.2.cloned.1.call-start = ((), (), s32[]{:S(2)}) async-start(), calls=%async_computation.8 | async-start | bytes 11059200 | tf_op jit(solution)/shard_map/reduce_scatter | solution.py:84
  113.7 1.0 copy-start.2
  114.7 12.6 %slice-start = ((bf16[3,128,1450]{1,2,0:T(8,128)(2,1)}), bf16[3,128,1440]{1,2,0:T(8,128)(2,1)S(1)}, s32[]{:S(2)}) async-start(bf16[3,128,1450]{1,2,0:T(8,128)(2,1)} %copy-done.2), calls=%async_computation.10 | async-start | bytes 2211840 | tf_op jit(solution)/shard_map/slice | solution.py:95
  146.5 72.2 %all-to-all-start.2 = ((bf16[8,240,1440]{2,1,0:T(8,128)(2,1)}), bf16[8,240,1440]{2,1,0:T(8,128)(2,1)}, u32[]{:S(2)}, u32[]{:S(2)}) async-start(bf16[8,240,1440]{2,1,0:T(8,128)(2,1)} %bitcast.135), calls=%async_computation.2 | async-start | bytes 11796480 | tf_op jit(solution)/shard_map/all_to_all | solution.py:22
  218.7 12.9 %all-to-all-start.1 = ((bf16[8,80,360]{2,1,0:T(8,128)(2,1)}), bf16[8,80,360]{2,1,0:T(8,128)(2,1)S(1)}, u32[]{:S(2)}, u32[]{:S(2)}) async-start(bf16[8,80,360]{2,1,0:T(8,128)(2,1)} %bitcast.14), calls=%async_computation.1 | async-start | bytes 983040 | tf_op jit(solution)/shard_map/all_to_all | solution.py:35
  230.7 6.6 %copy-start.6 = (s32[512]{0:T(512)S(1)}, s32[512]{0:T(512)}, u32[]{:S(2)}) copy-start(s32[512]{0:T(512)} %copy-done.5) | copy-start | bytes 6148
  231.6 24.3 %all-to-all-start.3 = ((bf16[8,240,360]{2,1,0:T(8,128)(2,1)}), bf16[8,240,360]{2,1,0:T(8,128)(2,1)}, u32[]{:S(2)}, u32[]{:S(2)}) async-start(bf16[8,240,360]{2,1,0:T(8,128)(2,1)} %bitcast.140), calls=%async_computation.3 | async-start | bytes 2949120 | tf_op jit(solution)/shard_map/all_to_all | solution.py:35
  279.1 40.1 %copy-start.1 = (bf16[128,4,1440]{0,2,1:T(8,128)(2,1)S(1)}, bf16[128,4,1440]{0,2,1:T(8,128)(2,1)}, u32[]{:S(2)}) copy-start(bf16[128,4,1440]{0,2,1:T(8,128)(2,1)} %param.7) | copy-start | bytes 4423684
  319.2 1.7 copy-start.8
Sparse Core Ops, SparseCore 0:
  39.8 37.5 all-gather.2
  108.6 152.0 reduce-scatter.1
where the time goes:
time: 335 us; the launch traced here: 333 us
  waiting for transfers between devices  109 us (33%)
  local copies, waits for them, and re-layouts  74.3 us (22%)
  blocking collectives  40.1 us (12%)
  matrix products  36.5 us (11%)
  starting transfers between devices  31.2 us (9%)
  other arithmetic  25.5 us (8%)
  between operations  15.7 us (5%)
    all_to_all x2, waiting for transfers between devices, dispatch(): lax.all_to_all(dy_buf.reshape(n_exp, per_dest, -1), 'exp', 0, 0, tiled=True)  70.4 us
    all_to_all x1, blocking collectives, body(): lax.all_to_all(proj_slot, 'grp', split_axis=0, concat_axis=0, tiled=True)  40.1 us
    all_to_all x2, waiting for transfers between devices, proj_home(): lax.all_to_all(proj.astype(jnp.bfloat16).reshape(n_exp, n * exp_dev * mos...  18.6 us
    all_to_all x1, waiting for transfers between devices, dispatch(): lax.all_to_all(hid_buf.reshape(n_exp, per_dest, -1), 'exp', 0, 0, tiled=T...  14.6 us
    all_to_all x2, starting transfers between devices, dispatch(): lax.all_to_all(dy_buf.reshape(n_exp, per_dest, -1), 'exp', 0, 0, tiled=True)  11.9 us
    all_to_all x2, starting transfers between devices, proj_home(): lax.all_to_all(proj.astype(jnp.bfloat16).reshape(n_exp, n * exp_dev * mos...  10.6 us
    dot_general x1, matrix products, body(): jnp.einsum('sjmgf,sjmd->gjfd', hid_a.reshape(n_exp, exp_dev, most, n_grp,...  10.5 us
    dot_general x2, matrix products, proj_home(): jnp.einsum('cgjmd,jfd->cgjmf', dy_r, w_down, preferred_element_type=jnp.f...  8.59 us
  transfers between devices with their start and end apart: 8, of which 6 were waited for; matrix products, arithmetic and copies ran while one was open for 32% of the time, Pallas kernels for 0%

commit v1 on v0

--- a/solution.py
+++ b/solution.py
@@ -6,12 +6,15 @@
 LOSS_SCALE = 32768
 
 
-def dispatch(ids, wt, cot, hid, experts, exp_dev, most, n_exp):
+def rank_of(ids, experts):
+    onehot = (ids[:, :, None] == jnp.arange(experts, dtype=jnp.int32)).astype(jnp.int32)
+    return jnp.sum((jnp.cumsum(onehot, axis=1) - onehot) * onehot, axis=2)
+
+
+def dispatch(ids, rank, wt, cot, hid, exp_dev, most, n_exp):
     n, per = ids.shape
     top = per * n // cot.shape[0]
     rows = n_exp * n * exp_dev * most
-    onehot = (ids[:, :, None] == jnp.arange(experts, dtype=jnp.int32)).astype(jnp.int32)
-    rank = jnp.sum((jnp.cumsum(onehot, axis=1) - onehot) * onehot, axis=2)
     src = jnp.arange(n, dtype=jnp.int32)[:, None]
     target = ((((ids // exp_dev) * n + src) * exp_dev + ids % exp_dev) * most + rank).reshape(-1)
     pick = (target[None, :] == jnp.arange(rows, dtype=jnp.int32)[:, None]).astype(jnp.bfloat16)
@@ -54,18 +57,26 @@
     live = (first_row + jnp.arange(tok, dtype=jnp.int32) < count).astype(jnp.float32)
     weighted = (gates.astype(jnp.float32) * live[:, None]).astype(jnp.bfloat16)
 
+    rank_own = rank_of(expert_ids.reshape(1, tok * top), experts)
     digits = jnp.stack([count // 64, count % 64]).astype(jnp.bfloat16)
     packed = jnp.concatenate(
-        [cotangent, expert_ids.astype(jnp.bfloat16), weighted, jnp.broadcast_to(digits, (tok, 2))], axis=1
+        [
+            cotangent,
+            expert_ids.astype(jnp.bfloat16),
+            weighted,
+            jnp.broadcast_to(digits, (tok, 2)),
+            rank_own.reshape(tok, top).astype(jnp.bfloat16),
+        ],
+        axis=1,
     )
     got = lax.all_gather(packed, "grp")
-    dig = got[:, 0, width + 2 * top :].astype(jnp.float32)
+    dig = got[:, 0, width + 2 * top : width + 2 * top + 2].astype(jnp.float32)
     total = jnp.sum(dig[:, 0] * 64.0 + dig[:, 1])
     scale = LOSS_SCALE / total
 
     pick_a, dy_a, gate_a, hid_a = dispatch(
-        expert_ids.reshape(1, tok * top), weighted.reshape(-1), cotangent,
-        hidden.reshape(tok * top, ffw), experts, exp_dev, most, n_exp,
+        expert_ids.reshape(1, tok * top), rank_own, weighted.reshape(-1), cotangent,
+        hidden.reshape(tok * top, ffw), exp_dev, most, n_exp,
     )
     gate_fa = gate_a.reshape(n_exp, exp_dev, most).astype(jnp.float32)
     dy_fa = dy_a.reshape(n_exp, exp_dev, most, width)
@@ -91,9 +102,10 @@
     n_b = n_grp - 1
     pick_b, dy_b, _, _ = dispatch(
         got_b[:, :, width : width + top].astype(jnp.int32).reshape(n_b, tok * top),
+        got_b[:, :, width + 2 * top + 2 :].astype(jnp.int32).reshape(n_b, tok * top),
         got_b[:, :, width + top : width + 2 * top].reshape(-1),
         got_b[:, :, :width].reshape(n_b * tok, width),
-        None, experts, exp_dev, most, n_exp,
+        None, exp_dev, most, n_exp,
     )
 
     proj_rel = jnp.concatenate(

time: 335 us -> 322 us (0.961)
  other arithmetic: 25.5 us -> 17.3 us
    another operation x4 -> x2, other arithmetic: 8.5 us -> 1.18 us
  transfers between devices with their start and end apart: 8 -> 8, of which waited for: 6 -> 6; matrix products, arithmetic and copies ran while one was open for 32% -> 30% of each run, Pallas kernels for 0% -> 0%
where the time goes in v1:
time: 322 us; the launch traced here: 320 us
  waiting for transfers between devices  108 us (34%)
  local copies, waits for them, and re-layouts  71.3 us (22%)
  blocking collectives  39.9 us (12%)
  matrix products  36.5 us (11%)
  starting transfers between devices  31.4 us (10%)
  other arithmetic  17.3 us (5%)
  between operations  15.7 us (5%)
    all_to_all x2, waiting for transfers between devices, dispatch(): lax.all_to_all(dy_buf.reshape(n_exp, per_dest, -1), 'exp', 0, 0, tiled=True)  70 us
    all_to_all x1, blocking collectives, body(): lax.all_to_all(proj_slot, 'grp', split_axis=0, concat_axis=0, tiled=True)  39.9 us
    all_to_all x2, waiting for transfers between devices, proj_home(): lax.all_to_all(proj.astype(jnp.bfloat16).reshape(n_exp, n * exp_dev * mos...  17.5 us
    all_to_all x1, waiting for transfers between devices, dispatch(): lax.all_to_all(hid_buf.reshape(n_exp, per_dest, -1), 'exp', 0, 0, tiled=T...  14.5 us
    all_to_all x2, starting transfers between devices, dispatch(): lax.all_to_all(dy_buf.reshape(n_exp, per_dest, -1), 'exp', 0, 0, tiled=True)  12.1 us
    all_to_all x2, starting transfers between devices, proj_home(): lax.all_to_all(proj.astype(jnp.bfloat16).reshape(n_exp, n * exp_dev * mos...  10.6 us
    dot_general x1, matrix products, body(): jnp.einsum('sjmgf,sjmd->gjfd', hid_a.reshape(n_exp, exp_dev, most, n_grp,...  10.4 us
    dot_general x2, matrix products, proj_home(): jnp.einsum('cgjmd,jfd->cgjmf', dy_r, w_down, preferred_element_type=jnp.f...  8.59 us
  transfers between devices with their start and end apart: 8, of which 6 were waited for; matrix products, arithmetic and copies ran while one was open for 30% of the time, Pallas kernels for 0%

profile of v1, /device:TPU:2, one launch (start us, length us, event | category | flops | bytes accessed | tf_op | source)
XLA Modules:
  0.0 320.0 jit_solution(12270727628706878794)
XLA Ops:
  7.2 0.9 copy.154
  8.3 1.2 reduce-window.6
  9.4 0.2 slice_reduce_fusion
  10.3 0.7 fusion.87
  11.0 0.1 copy.183
  11.6 0.3 fusion.42
  11.9 0.7 all_to_all.32
  12.6 4.3 %all-to-all-start.5 = ((bf16[8,1,80]{2,1,0:T(2,128)(2,1)}), bf16[8,1,80]{2,1,0:T(2,128)(2,1)S(1)}, u32[]{:S(2)}, u32[]{:S(2)}) async-start(bf16[8,1,80]{2,1,0:T(2,128)(2,1)} %all_to_all.32), calls=%async_computation.5 | async-start | bytes 8192 | tf_op jit(solution)/shard_map/all_to_all | solution.py:26
  16.9 3.8 %copy.185 = bf16[128,4,1440]{2,1,0:T(4,128)(2,1)} copy(bf16[128,4,1440]{0,2,1:T(8,128)(2,1)} %param.7) | data formatting | bytes 2949120 | tf_op args[1]
  20.7 3.7 %reshape.537 = bf16[512,1440]{1,0:T(8,128)(2,1)} reshape(bf16[128,4,1440]{2,1,0:T(4,128)(2,1)} %copy.185) | data formatting | bytes 2949120 | tf_op jit(solution)/shard_map/reshape | solution.py:79
  24.4 4.0 %convolution_convert_fusion.2 = bf16[640,1440]{0,1:T(8,128)(2,1)} fusion(bf16[512,1440]{1,0:T(8,128)(2,1)} %reshape.537, s32[512]{0:T(512)S(1)} %fusion.78), kind=kOutput, calls=%fused_computation.16 | convolution fusion | flops 944967680 | bytes 3319808 | tf_op jit(solution)/shard_map/dot_general | solution.py:29
  28.4 3.9 %copy.186 = bf16[640,1440]{1,0:T(8,128)(2,1)} copy(bf16[640,1440]{0,1:T(8,128)(2,1)} %convolution_convert_fusion.2) | data formatting | bytes 3686400 | tf_op jit(solution)/shard_map/convert_element_type | solution.py:29
  32.4 4.4 %all-to-all-start.6 = ((bf16[8,80,1440]{2,1,0:T(8,128)(2,1)}), bf16[8,80,1440]{2,1,0:T(8,128)(2,1)}, u32[]{:S(2)}, u32[]{:S(2)}) async-start(bf16[8,80,1440]{2,1,0:T(8,128)(2,1)} %bitcast.119), calls=%async_computation.6 | async-start | bytes 3932160 | tf_op jit(solution)/shard_map/all_to_all | solution.py:30
  37.1 0.1 copy.163
  37.5 2.6 concatenate.7
  40.2 0.2 fusion.43
  40.3 1.9 convolution_convert_fusion.1
  42.2 3.8 %copy.166 = bf16[640,1440]{1,0:T(8,128)(2,1)} copy(bf16[640,1440]{0,1:T(8,128)(2,1)} %convolution_convert_fusion.1) | data formatting | bytes 3686400 | tf_op jit(solution)/shard_map/convert_element_type | solution.py:23
  46.1 14.5 %all-to-all-done.6 = bf16[8,80,1440]{2,1,0:T(8,128)(2,1)} async-done(((bf16[8,80,1440]{2,1,0:T(8,128)(2,1)}), bf16[8,80,1440]{2,1,0:T(8,128)(2,1)}, u32[]{:S(2)}, u32[]{:S(2)}) %all-to-all-start.6) | async-done | bytes 1843232 | tf_op jit(solution)/shard_map/all_to_all | solution.py:30
  60.6 5.8 %all-to-all-start = ((bf16[8,80,1440]{2,1,0:T(8,128)(2,1)}), bf16[8,80,1440]{2,1,0:T(8,128)(2,1)}, u32[]{:S(2)}, u32[]{:S(2)}) async-start(bf16[8,80,1440]{2,1,0:T(8,128)(2,1)} %bitcast.120), calls=%async_computation | async-start | bytes 3932160 | tf_op jit(solution)/shard_map/all_to_all | solution.py:25
  66.5 5.4 %reshape.539 = bf16[8,2,40,4,360]{4,3,2,1,0:T(4,128)(2,1)} reshape(bf16[8,80,1440]{2,1,0:T(8,128)(2,1)} %all-to-all-done.6) | data formatting | bytes 3686400 | tf_op jit(solution)/shard_map/reshape | solution.py:87
  71.9 6.0 %all-gather.3.cloned.1.call-done = bf16[512,1454]{0,1:T(8,128)(2,1)} async-done(((bf16[128,1454]{0,1:T(8,128)(2,1)}), bf16[512,1454]{0,1:T(8,128)(2,1)}) %all-gather.3.cloned.1.call-update) | async-done | bytes 1488912 | tf_op jit(solution)/shard_map/all_gather | solution.py:72
  77.9 2.6 copy.170
  80.5 0.8 slice.40
  81.3 0.6 add_reduce_fusion
  82.6 7.6 %all-to-all-done = bf16[8,80,1440]{2,1,0:T(8,128)(2,1)} async-done(((bf16[8,80,1440]{2,1,0:T(8,128)(2,1)}), bf16[8,80,1440]{2,1,0:T(8,128)(2,1)}, u32[]{:S(2)}, u32[]{:S(2)}) %all-to-all-start) | async-done | bytes 1843232 | tf_op jit(solution)/shard_map/all_to_all | solution.py:25
  90.2 10.4 %fusion.3 = bf16[4,2,360,1440]{3,2,0,1:T(8,128)(2,1)} fusion(f32[]{:T(128)S(6)} %div.58, bf16[8,2,40,4,360]{4,3,2,1,0:T(4,128)(2,1)} %reshape.539, bf16[8,2,40,1440]{3,2,1,0:T(8,128)(2,1)} %bitcast.8, f32[8,2,40]{2,1,0:T(2,128)S(1)} %reshape.542), kind=kOutput, calls=%fused_computation.8 | convolution fusion | flops 2665267200 | bytes 11983364 | tf_op jit(solution)/shard_map/sjmgf,sjmd->gjfd/dot_general | solution.py:85
  100.7 7.8 %copy.190 = bf16[4,2,360,1440]{3,2,1,0:T(8,128)(2,1)} copy(bf16[4,2,360,1440]{3,2,0,1:T(8,128)(2,1)} %fusion.3) | data formatting | bytes 16588800 | tf_op jit(solution)/shard_map/convert_element_type | solution.py:93
  108.5 0.2 add.249
  108.9 2.6 copy.171
  111.5 2.1 gather_fusion
  113.6 0.2 broadcast_select_fusion.1
  113.8 1.0 copy-done.2
  114.9 1.7 copy.175
  116.6 0.7 fusion.71
  117.3 1.9 fusion.4
  119.2 6.6 %convolution_convert_fusion = bf16[1920,1440]{0,1:T(8,128)(2,1)} fusion(bf16[1920,384]{1,0:T(8,128)(2,1)S(1)} %fusion.4, bf16[384,1440]{1,0:T(8,128)(2,1)} %bitcast.125), kind=kOutput, calls=%fused_computation.9 | convolution fusion | flops 2126131200 | bytes 8110080 | tf_op jit(solution)/shard_map/dot_general | solution.py:23
  125.8 8.2 %copy.195 = bf16[1920,1440]{1,0:T(8,128)(2,1)} copy(bf16[1920,1440]{0,1:T(8,128)(2,1)} %convolution_convert_fusion) | data formatting | bytes 11059200 | tf_op jit(solution)/shard_map/reshape | solution.py:25
  134.0 6.3 %all-to-all-start.2 = ((bf16[8,240,1440]{2,1,0:T(8,128)(2,1)}), bf16[8,240,1440]{2,1,0:T(8,128)(2,1)}, u32[]{:S(2)}, u32[]{:S(2)}) async-start(bf16[8,240,1440]{2,1,0:T(8,128)(2,1)} %bitcast.118), calls=%async_computation.2 | async-start | bytes 11796480 | tf_op jit(solution)/shard_map/all_to_all | solution.py:25
  140.3 2.7 fusion.37
  143.0 0.8 copy.168
  143.9 62.4 %all-to-all-done.2 = bf16[8,240,1440]{2,1,0:T(8,128)(2,1)} async-done(((bf16[8,240,1440]{2,1,0:T(8,128)(2,1)}), bf16[8,240,1440]{2,1,0:T(8,128)(2,1)}, u32[]{:S(2)}, u32[]{:S(2)}) %all-to-all-start.2) | async-done | bytes 5529632 | tf_op jit(solution)/shard_map/all_to_all | solution.py:25
  206.3 4.9 %all-to-all-start.1 = ((bf16[8,80,360]{2,1,0:T(8,128)(2,1)}), bf16[8,80,360]{2,1,0:T(8,128)(2,1)S(1)}, u32[]{:S(2)}, u32[]{:S(2)}) async-start(bf16[8,80,360]{2,1,0:T(8,128)(2,1)} %bitcast.14), calls=%async_computation.1 | async-start | bytes 983040 | tf_op jit(solution)/shard_map/all_to_all | solution.py:38
  211.2 5.9 %fusion.23 = bf16[8,3,2,40,360]{4,3,1,0,2:T(8,128)(2,1)S(1)} fusion(bf16[2,360,1440]{2,1,0:T(8,128)(2,1)S(1)} %copy-done, bf16[8,3,2,40,1440]{4,3,2,1,0:T(8,128)(2,1)} %bitcast.24), kind=kOutput, calls=%fused_computation.32 | convolution fusion | flops 1991347200 | bytes 8985600 | tf_op jit(solution)/shard_map/cgjmd,jfd->cgjmf/dot_general | solution.py:37
  217.1 1.3 copy.178
  218.3 0.8 all-to-all-done.1
  219.1 5.7 %all-to-all-start.3 = ((bf16[8,240,360]{2,1,0:T(8,128)(2,1)}), bf16[8,240,360]{2,1,0:T(8,128)(2,1)}, u32[]{:S(2)}, u32[]{:S(2)}) async-start(bf16[8,240,360]{2,1,0:T(8,128)(2,1)} %bitcast.123), calls=%async_computation.3 | async-start | bytes 2949120 | tf_op jit(solution)/shard_map/all_to_all | solution.py:38
  224.9 0.5 fusion.36
  225.4 0.7 slice_convert_fusion.1
  226.3 0.1 reshape.527
  226.6 0.1 reshape.528
  226.7 16.7 %all-to-all-done.3 = bf16[8,240,360]{2,1,0:T(8,128)(2,1)} async-done(((bf16[8,240,360]{2,1,0:T(8,128)(2,1)}), bf16[8,240,360]{2,1,0:T(8,128)(2,1)}, u32[]{:S(2)}, u32[]{:S(2)}) %all-to-all-start.3) | async-done | bytes 1382432 | tf_op jit(solution)/shard_map/all_to_all | solution.py:38
  243.4 4.1 %fusion.10 = bf16[1536,360]{0,1:T(8,128)(2,1)S(1)} fusion(bf16[1920,360]{1,0:T(8,128)(2,1)} %bitcast.29, s32[1536]{0:T(1024)S(1)} %fusion.61), kind=kOutput, calls=%fused_computation.21 | convolution fusion | flops 2126868480 | bytes 2494464 | tf_op jit(solution)/shard_map/dot_general | solution.py:41
  247.5 1.3 pad_maximum_fusion
  248.8 2.6 copy.179
  251.3 3.9 %convert_element_type.164 = bf16[4,128,4,360]{3,2,1,0:T(4,128)(2,1)} reshape(bf16[2048,360]{1,0:T(8,128)(2,1)} %copy.179) | data formatting | bytes 2949120 | tf_op jit(solution)/shard_map/convert_element_type | solution.py:113
  255.2 2.8 copy.180
  258.0 3.3 %gather_fusion.1 = bf16[4,128,4,360]{3,1,2,0:T(8,128)(2,1)} fusion(bf16[4,128,4,360]{3,1,2,0:T(8,128)(2,1)} %copy.180, s32[1024]{0:T(1024)S(1)} %pad_clamp_fusion), kind=kCustom, calls=%fused_computation.1 | custom fusion | bytes 2949136 | tf_op jit(solution)/shard_map/jit(_take)/gather | solution.py:115
  261.3 2.8 broadcast_select_fusion
  264.1 2.6 copy.181
  266.7 39.9 %all_to_all.40 = bf16[4,128,4,360]{1,3,2,0:T(8,128)(2,1)S(1)} all-to-all(bf16[4,128,4,360]{1,3,2,0:T(8,128)(2,1)} %copy.181), channel_id=1, replica_groups=mesh['grp'=4,'exp'=8] {'grp'}, dimensions={0} | all-to-all | bytes 2949120 | tf_op jit(solution)/shard_map/all_to_all | solution.py:116
  306.6 1.7 fusion.9
  308.3 0.6 multiply_convert_fusion.1
  308.8 4.3 %convert.26 = f32[2,360,1440]{2,1,0:T(8,128)} convert(bf16[2,360,1440]{2,1,0:T(8,128)(2,1)} %bitcast.124) | non-fusion elementwise | flops 1036800 | bytes 6220800 | tf_op jit(solution)/shard_map/convert_element_type | solution.py:97
  (53 shorter events, 1.9 us)
Async XLA Ops:
  7.2 133.1 %copy-start = (bf16[2,360,1440]{2,1,0:T(8,128)(2,1)S(1)}, bf16[2,360,1440]{2,1,0:T(8,128)(2,1)}, u32[]{:S(2)}) copy-start(bf16[2,360,1440]{2,1,0:T(8,128)(2,1)} %param.11) | copy-start | bytes 6220804
  12.6 19.7 %all-to-all-start.5 = ((bf16[8,1,80]{2,1,0:T(2,128)(2,1)}), bf16[8,1,80]{2,1,0:T(2,128)(2,1)S(1)}, u32[]{:S(2)}, u32[]{:S(2)}) async-start(bf16[8,1,80]{2,1,0:T(2,128)(2,1)} %all_to_all.32), calls=%async_computation.5 | async-start | bytes 8192 | tf_op jit(solution)/shard_map/all_to_all | solution.py:26
  32.4 4.5 %copy-start.4 = (s32[128,4]{0,1:T(4,128)S(1)}, s32[128,4]{0,1:T(4,128)}, u32[]{:S(2)}) copy-start(s32[128,4]{0,1:T(4,128)} %param.9) | copy-start | bytes 6148
  32.4 5.2 %copy-start.3 = (bf16[128,1440]{0,1:T(8,128)(2,1)S(1)}, bf16[128,1440]{0,1:T(8,128)(2,1)}, u32[]{:S(2)}) copy-start(bf16[128,1440]{0,1:T(8,128)(2,1)} %param.6) | copy-start | bytes 1105924
  32.4 28.2 %all-to-all-start.6 = ((bf16[8,80,1440]{2,1,0:T(8,128)(2,1)}), bf16[8,80,1440]{2,1,0:T(8,128)(2,1)}, u32[]{:S(2)}, u32[]{:S(2)}) async-start(bf16[8,80,1440]{2,1,0:T(8,128)(2,1)} %bitcast.119), calls=%async_computation.6 | async-start | bytes 3932160 | tf_op jit(solution)/shard_map/all_to_all | solution.py:30
  36.8 41.1 %all-gather.3.cloned.1.call-start = ((), (), s32[]{:S(2)}) async-start(), calls=%async_computation.9 | async-start | bytes 1863680 | tf_op jit(solution)/shard_map/all_gather | solution.py:72
  60.6 29.6 %all-to-all-start = ((bf16[8,80,1440]{2,1,0:T(8,128)(2,1)}), bf16[8,80,1440]{2,1,0:T(8,128)(2,1)}, u32[]{:S(2)}, u32[]{:S(2)}) async-start(bf16[8,80,1440]{2,1,0:T(8,128)(2,1)} %bitcast.120), calls=%async_computation | async-start | bytes 3932160 | tf_op jit(solution)/shard_map/all_to_all | solution.py:25
  66.4 242.5 %reduce-scatter.2.cloned.1.call-start = ((), (), s32[]{:S(2)}) async-start(), calls=%async_computation.8 | async-start | bytes 11059200 | tf_op jit(solution)/shard_map/reduce_scatter | solution.py:95
  113.8 1.0 copy-start.2
  134.0 72.3 %all-to-all-start.2 = ((bf16[8,240,1440]{2,1,0:T(8,128)(2,1)}), bf16[8,240,1440]{2,1,0:T(8,128)(2,1)}, u32[]{:S(2)}, u32[]{:S(2)}) async-start(bf16[8,240,1440]{2,1,0:T(8,128)(2,1)} %bitcast.118), calls=%async_computation.2 | async-start | bytes 11796480 | tf_op jit(solution)/shard_map/all_to_all | solution.py:25
  206.3 12.9 %all-to-all-start.1 = ((bf16[8,80,360]{2,1,0:T(8,128)(2,1)}), bf16[8,80,360]{2,1,0:T(8,128)(2,1)S(1)}, u32[]{:S(2)}, u32[]{:S(2)}) async-start(bf16[8,80,360]{2,1,0:T(8,128)(2,1)} %bitcast.14), calls=%async_computation.1 | async-start | bytes 983040 | tf_op jit(solution)/shard_map/all_to_all | solution.py:38
  219.1 24.2 %all-to-all-start.3 = ((bf16[8,240,360]{2,1,0:T(8,128)(2,1)}), bf16[8,240,360]{2,1,0:T(8,128)(2,1)}, u32[]{:S(2)}, u32[]{:S(2)}) async-start(bf16[8,240,360]{2,1,0:T(8,128)(2,1)} %bitcast.123), calls=%async_computation.3 | async-start | bytes 2949120 | tf_op jit(solution)/shard_map/all_to_all | solution.py:38
  266.7 39.9 %copy-start.1 = (bf16[128,4,1440]{0,2,1:T(8,128)(2,1)S(1)}, bf16[128,4,1440]{0,2,1:T(8,128)(2,1)}, u32[]{:S(2)}) copy-start(bf16[128,4,1440]{0,2,1:T(8,128)(2,1)} %param.7) | copy-start | bytes 4423684
Sparse Core Ops, SparseCore 0:
  40.2 37.6 all-gather.2
  108.6 152.0 reduce-scatter.1

commit v2 on v1

--- a/solution.py
+++ b/solution.py
@@ -83,19 +83,17 @@
     scaled = (gate_fa[..., None] * dy_fa.astype(jnp.float32)).astype(jnp.bfloat16)
     partial_grad = (
         jnp.einsum(
-            "sjmgf,sjmd->gjfd",
+            "sjmgf,sjmd->jgfd",
             hid_a.reshape(n_exp, exp_dev, most, n_grp, f_loc),
             scaled,
             preferred_element_type=jnp.float32,
         )
         * scale
     )
-    grad_rows = partial_grad.astype(jnp.bfloat16).reshape(n_grp * exp_dev * f_loc, width)
-    d_weight = (
-        lax.psum_scatter(grad_rows, "grp", scatter_dimension=0, tiled=True)
-        .reshape(exp_dev, f_loc, width)
-        .astype(jnp.float32)
-    )
+    grad_rows = partial_grad.astype(jnp.bfloat16).reshape(exp_dev, n_grp * f_loc, width)
+    d_weight = jnp.stack(
+        [lax.psum_scatter(grad_rows[j], "grp", scatter_dimension=0, tiled=True) for j in range(exp_dev)]
+    ).astype(jnp.float32)
 
     rel = (me + jnp.arange(1, n_grp, dtype=jnp.int32)) % n_grp
     got_b = jnp.take(got, rel, axis=0)

time: 322 us -> 314 us (0.975)
  local copies, waits for them, and re-layouts: 71.3 us -> 67.6 us
  matrix products: 36.5 us -> 32.9 us
    convert_element_type x1 -> x0, local copies, waits for them, and re-layouts: 7.83 us -> none  [body(): partial_grad.astype(jnp.bfloat16).reshape(n_grp * exp_dev * f_loc, width)]
    slice x1 -> x2, local copies, waits for them, and re-layouts: 0.22 us -> 4.01 us  [the longest x1 3.8 us: body(): grad_rows[j]]
    dot_general x1, matrix products: 10.4 us -> 7.04 us  [body(): jnp.einsum('sjmgf,sjmd->jgfd', hid_a.reshape(n_exp, exp_dev, most, n_grp,...]
  transfers between devices with their start and end apart: 8 -> 9, of which waited for: 6 -> 6; matrix products, arithmetic and copies ran while one was open for 30% -> 31% of each run, Pallas kernels for 0% -> 0%
where the time goes in v2:
time: 314 us; the launch traced here: 312 us
  waiting for transfers between devices  108 us (34%)
  local copies, waits for them, and re-layouts  67.6 us (22%)
  blocking collectives  39.9 us (13%)
  matrix products  32.9 us (10%)
  starting transfers between devices  31.2 us (10%)
  other arithmetic  17 us (5%)
  between operations  15.4 us (5%)
    all_to_all x2, waiting for transfers between devices, dispatch(): lax.all_to_all(dy_buf.reshape(n_exp, per_dest, -1), 'exp', 0, 0, tiled=True)  69.3 us
    all_to_all x1, blocking collectives, body(): lax.all_to_all(proj_slot, 'grp', split_axis=0, concat_axis=0, tiled=True)  39.9 us
    all_to_all x2, waiting for transfers between devices, proj_home(): lax.all_to_all(proj.astype(jnp.bfloat16).reshape(n_exp, n * exp_dev * mos...  17.5 us
    all_to_all x1, waiting for transfers between devices, dispatch(): lax.all_to_all(hid_buf.reshape(n_exp, per_dest, -1), 'exp', 0, 0, tiled=T...  14.5 us
    all_to_all x2, starting transfers between devices, dispatch(): lax.all_to_all(dy_buf.reshape(n_exp, per_dest, -1), 'exp', 0, 0, tiled=True)  11.9 us
    all_to_all x2, starting transfers between devices, proj_home(): lax.all_to_all(proj.astype(jnp.bfloat16).reshape(n_exp, n * exp_dev * mos...  10.6 us
    dot_general x2, matrix products, proj_home(): jnp.einsum('cgjmd,jfd->cgjmf', dy_r, w_down, preferred_element_type=jnp.f...  8.59 us
    reshape x1, local copies, waits for them, and re-layouts, dispatch(): dy_buf.reshape(n_exp, per_dest, -1)  8.4 us
  transfers between devices with their start and end apart: 9, of which 6 were waited for; matrix products, arithmetic and copies ran while one was open for 31% of the time, Pallas kernels for 0%

profile of v2, /device:TPU:2, one launch (start us, length us, event | category | flops | bytes accessed | tf_op | source)
XLA Modules:
  0.0 311.9 jit_solution(16887602260328187384)
XLA Ops:
  7.2 0.9 copy.150
  8.3 1.2 reduce-window.6
  9.4 0.2 slice_reduce_fusion
  10.3 0.7 fusion.86
  11.6 0.3 fusion.41
  11.9 0.7 all_to_all.32
  12.6 4.3 %all-to-all-start.6 = ((bf16[8,1,80]{2,1,0:T(2,128)(2,1)}), bf16[8,1,80]{2,1,0:T(2,128)(2,1)S(1)}, u32[]{:S(2)}, u32[]{:S(2)}) async-start(bf16[8,1,80]{2,1,0:T(2,128)(2,1)} %all_to_all.32), calls=%async_computation.6 | async-start | bytes 8192 | tf_op jit(solution)/shard_map/all_to_all | solution.py:26
  16.9 3.8 %copy.179 = bf16[128,4,1440]{2,1,0:T(4,128)(2,1)} copy(bf16[128,4,1440]{0,2,1:T(8,128)(2,1)} %param.7) | data formatting | bytes 2949120 | tf_op args[1]
  20.7 3.7 %reshape.535 = bf16[512,1440]{1,0:T(8,128)(2,1)} reshape(bf16[128,4,1440]{2,1,0:T(4,128)(2,1)} %copy.179) | data formatting | bytes 2949120 | tf_op jit(solution)/shard_map/reshape | solution.py:79
  24.4 4.0 %convolution_convert_fusion.2 = bf16[640,1440]{0,1:T(8,128)(2,1)} fusion(bf16[512,1440]{1,0:T(8,128)(2,1)} %reshape.535, s32[512]{0:T(512)S(1)} %fusion.77), kind=kOutput, calls=%fused_computation.15 | convolution fusion | flops 944967680 | bytes 3319808 | tf_op jit(solution)/shard_map/dot_general | solution.py:29
  28.4 3.9 %copy.180 = bf16[640,1440]{1,0:T(8,128)(2,1)} copy(bf16[640,1440]{0,1:T(8,128)(2,1)} %convolution_convert_fusion.2) | data formatting | bytes 3686400 | tf_op jit(solution)/shard_map/convert_element_type | solution.py:29
  32.3 4.4 %all-to-all-start.5 = ((bf16[8,80,1440]{2,1,0:T(8,128)(2,1)}), bf16[8,80,1440]{2,1,0:T(8,128)(2,1)}, u32[]{:S(2)}, u32[]{:S(2)}) async-start(bf16[8,80,1440]{2,1,0:T(8,128)(2,1)} %bitcast.117), calls=%async_computation.5 | async-start | bytes 3932160 | tf_op jit(solution)/shard_map/all_to_all | solution.py:30
  37.0 0.1 copy.159
  37.5 2.6 concatenate.7
  40.1 0.2 fusion.42
  40.3 1.9 convolution_convert_fusion.1
  42.2 3.8 %copy.162 = bf16[640,1440]{1,0:T(8,128)(2,1)} copy(bf16[640,1440]{0,1:T(8,128)(2,1)} %convolution_convert_fusion.1) | data formatting | bytes 3686400 | tf_op jit(solution)/shard_map/convert_element_type | solution.py:23
  46.1 14.5 %all-to-all-done.5 = bf16[8,80,1440]{2,1,0:T(8,128)(2,1)} async-done(((bf16[8,80,1440]{2,1,0:T(8,128)(2,1)}), bf16[8,80,1440]{2,1,0:T(8,128)(2,1)}, u32[]{:S(2)}, u32[]{:S(2)}) %all-to-all-start.5) | async-done | bytes 1843232 | tf_op jit(solution)/shard_map/all_to_all | solution.py:30
  60.6 5.8 %all-to-all-start = ((bf16[8,80,1440]{2,1,0:T(8,128)(2,1)}), bf16[8,80,1440]{2,1,0:T(8,128)(2,1)}, u32[]{:S(2)}, u32[]{:S(2)}) async-start(bf16[8,80,1440]{2,1,0:T(8,128)(2,1)} %bitcast.118), calls=%async_computation | async-start | bytes 3932160 | tf_op jit(solution)/shard_map/all_to_all | solution.py:25
  66.4 5.4 %reshape.537 = bf16[8,2,40,4,360]{4,3,2,1,0:T(4,128)(2,1)} reshape(bf16[8,80,1440]{2,1,0:T(8,128)(2,1)} %all-to-all-done.5) | data formatting | bytes 3686400 | tf_op jit(solution)/shard_map/reshape | solution.py:87
  71.8 6.0 %all-gather.3.cloned.1.call-done = bf16[512,1454]{0,1:T(8,128)(2,1)} async-done(((bf16[128,1454]{0,1:T(8,128)(2,1)}), bf16[512,1454]{0,1:T(8,128)(2,1)}) %all-gather.3.cloned.1.call-update) | async-done | bytes 1488912 | tf_op jit(solution)/shard_map/all_gather | solution.py:72
  77.8 2.6 copy.166
  80.4 0.8 slice.50
  81.3 0.6 add_reduce_fusion
  82.6 7.6 %all-to-all-done = bf16[8,80,1440]{2,1,0:T(8,128)(2,1)} async-done(((bf16[8,80,1440]{2,1,0:T(8,128)(2,1)}), bf16[8,80,1440]{2,1,0:T(8,128)(2,1)}, u32[]{:S(2)}, u32[]{:S(2)}) %all-to-all-start) | async-done | bytes 1843232 | tf_op jit(solution)/shard_map/all_to_all | solution.py:25
  90.2 7.0 %fusion = bf16[2,4,360,1440]{3,2,1,0:T(8,128)(2,1)S(1)} fusion(f32[]{:T(128)S(6)} %div.58, bf16[8,2,40,4,360]{4,3,2,1,0:T(4,128)(2,1)} %reshape.537, bf16[8,2,40,1440]{3,2,1,0:T(8,128)(2,1)} %bitcast.8, f32[8,2,40]{2,1,0:T(2,128)S(1)} %reshape.540), kind=kOutput, calls=%fused_computation.3 | convolution fusion | flops 2665267200 | bytes 11983364 | tf_op jit(solution)/shard_map/sjmgf,sjmd->jgfd/dot_general | solution.py:85
  97.2 3.8 %fusion.87 = (bf16[1,4,360,1440]{3,2,1,0:T(8,128)(2,1)}, bf16[1,4,360,1440]{3,2,1,0:T(8,128)(2,1)}) fusion(bf16[2,4,360,1440]{3,2,1,0:T(8,128)(2,1)S(1)} %fusion), kind=kLoop, calls=%fused_computation.148 | loop fusion | bytes 16588800 | tf_op jit(solution)/shard_map/slice | solution.py:95
  101.1 0.2 add.251
  101.4 2.6 copy.167
  104.0 2.1 gather_fusion
  106.1 0.2 broadcast_select_fusion.1
  106.3 1.0 copy-done.2
  107.4 1.7 copy.171
  109.1 0.7 fusion.70
  109.8 1.9 fusion.3
  111.7 6.4 %convolution_convert_fusion = bf16[1920,1440]{0,1:T(8,128)(2,1)} fusion(bf16[1920,384]{1,0:T(8,128)(2,1)S(1)} %fusion.3, bf16[384,1440]{1,0:T(8,128)(2,1)} %bitcast.122), kind=kOutput, calls=%fused_computation.8 | convolution fusion | flops 2126131200 | bytes 8110080 | tf_op jit(solution)/shard_map/dot_general | solution.py:23
  118.1 8.4 %copy.190 = bf16[1920,1440]{1,0:T(8,128)(2,1)} copy(bf16[1920,1440]{0,1:T(8,128)(2,1)} %convolution_convert_fusion) | data formatting | bytes 11059200 | tf_op jit(solution)/shard_map/reshape | solution.py:25
  126.5 6.1 %all-to-all-start.2 = ((bf16[8,240,1440]{2,1,0:T(8,128)(2,1)}), bf16[8,240,1440]{2,1,0:T(8,128)(2,1)}, u32[]{:S(2)}, u32[]{:S(2)}) async-start(bf16[8,240,1440]{2,1,0:T(8,128)(2,1)} %bitcast.114), calls=%async_computation.2 | async-start | bytes 11796480 | tf_op jit(solution)/shard_map/all_to_all | solution.py:25
  132.6 0.7 reduce-scatter.3.cloned.1.call-update
  133.4 2.7 fusion.36
  136.1 0.8 copy.164
  136.9 61.7 %all-to-all-done.2 = bf16[8,240,1440]{2,1,0:T(8,128)(2,1)} async-done(((bf16[8,240,1440]{2,1,0:T(8,128)(2,1)}), bf16[8,240,1440]{2,1,0:T(8,128)(2,1)}, u32[]{:S(2)}, u32[]{:S(2)}) %all-to-all-start.2) | async-done | bytes 5529632 | tf_op jit(solution)/shard_map/all_to_all | solution.py:25
  198.6 4.9 %all-to-all-start.1 = ((bf16[8,80,360]{2,1,0:T(8,128)(2,1)}), bf16[8,80,360]{2,1,0:T(8,128)(2,1)S(1)}, u32[]{:S(2)}, u32[]{:S(2)}) async-start(bf16[8,80,360]{2,1,0:T(8,128)(2,1)} %bitcast.14), calls=%async_computation.1 | async-start | bytes 983040 | tf_op jit(solution)/shard_map/all_to_all | solution.py:38
  203.5 5.9 %fusion.22 = bf16[8,3,2,40,360]{4,3,1,0,2:T(8,128)(2,1)S(1)} fusion(bf16[2,360,1440]{2,1,0:T(8,128)(2,1)S(1)} %copy-done, bf16[8,3,2,40,1440]{4,3,2,1,0:T(8,128)(2,1)} %bitcast.24), kind=kOutput, calls=%fused_computation.32 | convolution fusion | flops 1991347200 | bytes 8985600 | tf_op jit(solution)/shard_map/cgjmd,jfd->cgjmf/dot_general | solution.py:37
  209.4 1.3 copy.174
  210.7 0.8 all-to-all-done.1
  211.5 5.6 %all-to-all-start.3 = ((bf16[8,240,360]{2,1,0:T(8,128)(2,1)}), bf16[8,240,360]{2,1,0:T(8,128)(2,1)}, u32[]{:S(2)}, u32[]{:S(2)}) async-start(bf16[8,240,360]{2,1,0:T(8,128)(2,1)} %bitcast.121), calls=%async_computation.3 | async-start | bytes 2949120 | tf_op jit(solution)/shard_map/all_to_all | solution.py:38
  217.2 0.5 fusion.35
  217.7 0.7 slice_convert_fusion.1
  218.6 0.1 reshape.526
  218.9 0.1 reshape.527
  219.1 16.7 %all-to-all-done.3 = bf16[8,240,360]{2,1,0:T(8,128)(2,1)} async-done(((bf16[8,240,360]{2,1,0:T(8,128)(2,1)}), bf16[8,240,360]{2,1,0:T(8,128)(2,1)}, u32[]{:S(2)}, u32[]{:S(2)}) %all-to-all-start.3) | async-done | bytes 1382432 | tf_op jit(solution)/shard_map/all_to_all | solution.py:38
  235.7 4.1 %fusion.9 = bf16[1536,360]{0,1:T(8,128)(2,1)S(1)} fusion(bf16[1920,360]{1,0:T(8,128)(2,1)} %bitcast.29, s32[1536]{0:T(1024)S(1)} %fusion.60), kind=kOutput, calls=%fused_computation.20 | convolution fusion | flops 2126868480 | bytes 2494464 | tf_op jit(solution)/shard_map/dot_general | solution.py:41
  239.8 1.3 pad_maximum_fusion
  241.1 2.6 copy.175
  243.7 3.9 %convert_element_type.158 = bf16[4,128,4,360]{3,2,1,0:T(4,128)(2,1)} reshape(bf16[2048,360]{1,0:T(8,128)(2,1)} %copy.175) | data formatting | bytes 2949120 | tf_op jit(solution)/shard_map/convert_element_type | solution.py:111
  247.6 2.9 copy.176
  250.5 3.3 %gather_fusion.1 = bf16[4,128,4,360]{3,1,2,0:T(8,128)(2,1)} fusion(bf16[4,128,4,360]{3,1,2,0:T(8,128)(2,1)} %copy.176, s32[1024]{0:T(1024)S(1)} %pad_clamp_fusion), kind=kCustom, calls=%fused_computation.1 | custom fusion | bytes 2949136 | tf_op jit(solution)/shard_map/jit(_take)/gather | solution.py:113
  253.8 2.9 broadcast_select_fusion
  256.7 2.6 copy.177
  259.2 39.9 %all_to_all.40 = bf16[4,128,4,360]{1,3,2,0:T(8,128)(2,1)S(1)} all-to-all(bf16[4,128,4,360]{1,3,2,0:T(8,128)(2,1)} %copy.177), channel_id=1, replica_groups=mesh['grp'=4,'exp'=8] {'grp'}, dimensions={0} | all-to-all | bytes 2949120 | tf_op jit(solution)/shard_map/all_to_all | solution.py:114
  299.2 1.7 fusion.8
  300.9 0.6 multiply_convert_fusion.1
  301.4 4.0 %maximum_convert_fusion = f32[2,360,1440]{2,1,0:T(8,128)} fusion(bf16[1,360,1440]{2,1,0:T(8,128)(2,1)} %bitcast.123, bf16[1,360,1440]{2,1,0:T(8,128)(2,1)} %bitcast.124), kind=kLoop, calls=%fused_computation.21 | loop fusion | flops 2073600 | bytes 6220800 | tf_op jit(solution)/shard_map/convert_element_type | solution.py:96
  (56 shorter events, 2.1 us)
Async XLA Ops:
  7.2 126.2 %copy-start = (bf16[2,360,1440]{2,1,0:T(8,128)(2,1)S(1)}, bf16[2,360,1440]{2,1,0:T(8,128)(2,1)}, u32[]{:S(2)}) copy-start(bf16[2,360,1440]{2,1,0:T(8,128)(2,1)} %param.11) | copy-start | bytes 6220804
  12.6 19.7 %all-to-all-start.6 = ((bf16[8,1,80]{2,1,0:T(2,128)(2,1)}), bf16[8,1,80]{2,1,0:T(2,128)(2,1)S(1)}, u32[]{:S(2)}, u32[]{:S(2)}) async-start(bf16[8,1,80]{2,1,0:T(2,128)(2,1)} %all_to_all.32), calls=%async_computation.6 | async-start | bytes 8192 | tf_op jit(solution)/shard_map/all_to_all | solution.py:26
  32.3 4.5 %copy-start.4 = (s32[128,4]{0,1:T(4,128)S(1)}, s32[128,4]{0,1:T(4,128)}, u32[]{:S(2)}) copy-start(s32[128,4]{0,1:T(4,128)} %param.9) | copy-start | bytes 6148
  32.3 5.2 %copy-start.3 = (bf16[128,1440]{0,1:T(8,128)(2,1)S(1)}, bf16[128,1440]{0,1:T(8,128)(2,1)}, u32[]{:S(2)}) copy-start(bf16[128,1440]{0,1:T(8,128)(2,1)} %param.6) | copy-start | bytes 1105924
  32.3 28.2 %all-to-all-start.5 = ((bf16[8,80,1440]{2,1,0:T(8,128)(2,1)}), bf16[8,80,1440]{2,1,0:T(8,128)(2,1)}, u32[]{:S(2)}, u32[]{:S(2)}) async-start(bf16[8,80,1440]{2,1,0:T(8,128)(2,1)} %bitcast.117), calls=%async_computation.5 | async-start | bytes 3932160 | tf_op jit(solution)/shard_map/all_to_all | solution.py:30
  36.8 41.0 %all-gather.3.cloned.1.call-start = ((), (), s32[]{:S(2)}) async-start(), calls=%async_computation.11 | async-start | bytes 1863680 | tf_op jit(solution)/shard_map/all_gather | solution.py:72
  60.6 29.6 %all-to-all-start = ((bf16[8,80,1440]{2,1,0:T(8,128)(2,1)}), bf16[8,80,1440]{2,1,0:T(8,128)(2,1)}, u32[]{:S(2)}, u32[]{:S(2)}) async-start(bf16[8,80,1440]{2,1,0:T(8,128)(2,1)} %bitcast.118), calls=%async_computation | async-start | bytes 3932160 | tf_op jit(solution)/shard_map/all_to_all | solution.py:25
  66.3 235.1 %reduce-scatter.5.cloned.1.call-start = ((), (), s32[]{:S(2)}) async-start(), calls=%async_computation.10 | async-start | bytes 5529600 | tf_op jit(solution)/shard_map/reduce_scatter | solution.py:95
  106.3 1.0 copy-start.2
  126.5 72.1 %all-to-all-start.2 = ((bf16[8,240,1440]{2,1,0:T(8,128)(2,1)}), bf16[8,240,1440]{2,1,0:T(8,128)(2,1)}, u32[]{:S(2)}, u32[]{:S(2)}) async-start(bf16[8,240,1440]{2,1,0:T(8,128)(2,1)} %bitcast.114), calls=%async_computation.2 | async-start | bytes 11796480 | tf_op jit(solution)/shard_map/all_to_all | solution.py:25
  132.6 168.8 %reduce-scatter.3.cloned.1.call-start = ((), (), s32[]{:S(2)}) async-start(), calls=%async_computation.9 | async-start | bytes 5529600 | tf_op jit(solution)/shard_map/reduce_scatter | solution.py:95
  198.6 12.9 %all-to-all-start.1 = ((bf16[8,80,360]{2,1,0:T(8,128)(2,1)}), bf16[8,80,360]{2,1,0:T(8,128)(2,1)S(1)}, u32[]{:S(2)}, u32[]{:S(2)}) async-start(bf16[8,80,360]{2,1,0:T(8,128)(2,1)} %bitcast.14), calls=%async_computation.1 | async-start | bytes 983040 | tf_op jit(solution)/shard_map/all_to_all | solution.py:38
  211.5 24.2 %all-to-all-start.3 = ((bf16[8,240,360]{2,1,0:T(8,128)(2,1)}), bf16[8,240,360]{2,1,0:T(8,128)(2,1)}, u32[]{:S(2)}, u32[]{:S(2)}) async-start(bf16[8,240,360]{2,1,0:T(8,128)(2,1)} %bitcast.121), calls=%async_computation.3 | async-start | bytes 2949120 | tf_op jit(solution)/shard_map/all_to_all | solution.py:38
  259.2 40.0 %copy-start.1 = (bf16[128,4,1440]{0,2,1:T(8,128)(2,1)S(1)}, bf16[128,4,1440]{0,2,1:T(8,128)(2,1)}, u32[]{:S(2)}) copy-start(bf16[128,4,1440]{0,2,1:T(8,128)(2,1)} %param.7) | copy-start | bytes 4423684
Sparse Core Ops, SparseCore 0:
  40.2 37.5 all-gather.2
  101.2 80.8 reduce-scatter.4
  185.0 80.9 reduce-scatter.2

commit v3 on v2

--- a/solution.py
+++ b/solution.py
@@ -11,7 +11,7 @@
     return jnp.sum((jnp.cumsum(onehot, axis=1) - onehot) * onehot, axis=2)
 
 
-def dispatch(ids, rank, wt, cot, hid, exp_dev, most, n_exp):
+def dispatch(ids, rank, wt, cot, hid, exp_dev, most, n_exp, gather_rows=False):
     n, per = ids.shape
     top = per * n // cot.shape[0]
     rows = n_exp * n * exp_dev * most
@@ -20,7 +20,12 @@
     pick = (target[None, :] == jnp.arange(rows, dtype=jnp.int32)[:, None]).astype(jnp.bfloat16)
     pick_tok = jnp.sum(pick.reshape(rows, n * per // top, top), axis=2)
     per_dest = n * exp_dev * most
-    dy_buf = jnp.dot(pick_tok, cot, preferred_element_type=jnp.float32).astype(jnp.bfloat16)
+    if gather_rows:
+        tok_ids = jnp.arange(pick_tok.shape[1], dtype=jnp.float32)
+        row_tok = jnp.dot(pick_tok.astype(jnp.float32), tok_ids, precision=lax.Precision.HIGHEST)
+        dy_buf = jnp.take(cot, row_tok.astype(jnp.int32), axis=0)
+    else:
+        dy_buf = jnp.dot(pick_tok, cot, preferred_element_type=jnp.float32).astype(jnp.bfloat16)
     gate_buf = jnp.dot(pick, wt, preferred_element_type=jnp.float32).astype(jnp.bfloat16)
     dy_r = lax.all_to_all(dy_buf.reshape(n_exp, per_dest, -1), "exp", 0, 0, tiled=True)
     gate_r = lax.all_to_all(gate_buf.reshape(n_exp, per_dest), "exp", 0, 0, tiled=True)
@@ -103,7 +108,7 @@
         got_b[:, :, width + 2 * top + 2 :].astype(jnp.int32).reshape(n_b, tok * top),
         got_b[:, :, width + top : width + 2 * top].reshape(-1),
         got_b[:, :, :width].reshape(n_b * tok, width),
-        None, exp_dev, most, n_exp,
+        None, exp_dev, most, n_exp, gather_rows=True,
     )
 
     proj_rel = jnp.concatenate(

time: 314 us -> 315 us (level)
  other arithmetic: 17 us -> 22.8 us
  matrix products: 32.9 us -> 27.8 us
    reshape x2 -> x1, local copies, waits for them, and re-layouts: 8.41 us -> 0.01 us  [the longest x1 8.4 us: dispatch(): dy_buf.reshape(n_exp, per_dest, -1)]
    gather x0 -> x1, local copies, waits for them, and re-layouts: none -> 7.77 us  [dispatch(): dy_buf = jnp.take(cot, row_tok.astype(jnp.int32), axis=0)]
    dot_general x2 -> x1, matrix products: 8.31 us -> 1.91 us  [dispatch(): jnp.dot(pick_tok, cot, preferred_element_type=jnp.float32)]
    select_n x0 -> x2, other arithmetic: none -> 5.9 us  [dispatch(): dy_buf = jnp.take(cot, row_tok.astype(jnp.int32), axis=0)]
where the time goes in v3:
time: 315 us; the launch traced here: 313 us
  waiting for transfers between devices  108 us (34%)
  local copies, waits for them, and re-layouts  67.9 us (22%)
  blocking collectives  40 us (13%)
  starting transfers between devices  31 us (10%)
  matrix products  27.8 us (9%)
  other arithmetic  22.8 us (7%)
  between operations  15.4 us (5%)
    all_to_all x2, waiting for transfers between devices, dispatch(): lax.all_to_all(dy_buf.reshape(n_exp, per_dest, -1), 'exp', 0, 0, tiled=True)  69.3 us
    all_to_all x1, blocking collectives, body(): lax.all_to_all(proj_slot, 'grp', split_axis=0, concat_axis=0, tiled=True)  40 us
    all_to_all x2, waiting for transfers between devices, proj_home(): lax.all_to_all(proj.astype(jnp.bfloat16).reshape(n_exp, n * exp_dev * mos...  17.5 us
    all_to_all x1, waiting for transfers between devices, dispatch(): lax.all_to_all(hid_buf.reshape(n_exp, per_dest, -1), 'exp', 0, 0, tiled=T...  14.5 us
    all_to_all x2, starting transfers between devices, dispatch(): lax.all_to_all(dy_buf.reshape(n_exp, per_dest, -1), 'exp', 0, 0, tiled=True)  11.8 us
    all_to_all x2, starting transfers between devices, proj_home(): lax.all_to_all(proj.astype(jnp.bfloat16).reshape(n_exp, n * exp_dev * mos...  10.6 us
    dot_general x2, matrix products, proj_home(): jnp.einsum('cgjmd,jfd->cgjmf', dy_r, w_down, preferred_element_type=jnp.f...  8.61 us
    gather x1, local copies, waits for them, and re-layouts, dispatch(): dy_buf = jnp.take(cot, row_tok.astype(jnp.int32), axis=0)  7.77 us
  transfers between devices with their start and end apart: 9, of which 6 were waited for; matrix products, arithmetic and copies ran while one was open for 31% of the time, Pallas kernels for 0%

profile of v3, /device:TPU:2, one launch (start us, length us, event | category | flops | bytes accessed | tf_op | source)
XLA Modules:
  0.0 313.0 jit_solution(16177655674602957754)
XLA Ops:
  7.2 0.9 copy.142
  8.3 1.2 reduce-window.6
  9.4 0.2 slice_reduce_fusion
  10.3 0.7 fusion.87
  11.6 0.3 fusion.41
  11.9 0.7 all_to_all.32
  12.6 4.3 %all-to-all-start.6 = ((bf16[8,1,80]{2,1,0:T(2,128)(2,1)}), bf16[8,1,80]{2,1,0:T(2,128)(2,1)S(1)}, u32[]{:S(2)}, u32[]{:S(2)}) async-start(bf16[8,1,80]{2,1,0:T(2,128)(2,1)} %all_to_all.32), calls=%async_computation.6 | async-start | bytes 8192 | tf_op jit(solution)/shard_map/all_to_all | solution.py:31
  16.9 3.8 %copy.170 = bf16[128,4,1440]{2,1,0:T(4,128)(2,1)} copy(bf16[128,4,1440]{0,2,1:T(8,128)(2,1)} %param.7) | data formatting | bytes 2949120 | tf_op args[1]
  20.7 3.7 %reshape.543 = bf16[512,1440]{1,0:T(8,128)(2,1)} reshape(bf16[128,4,1440]{2,1,0:T(4,128)(2,1)} %copy.170) | data formatting | bytes 2949120 | tf_op jit(solution)/shard_map/reshape | solution.py:84
  24.4 4.0 %convolution_convert_fusion.1 = bf16[640,1440]{0,1:T(8,128)(2,1)} fusion(bf16[512,1440]{1,0:T(8,128)(2,1)} %reshape.543, s32[512]{0:T(512)S(1)} %fusion.77), kind=kOutput, calls=%fused_computation.16 | convolution fusion | flops 944967680 | bytes 3319808 | tf_op jit(solution)/shard_map/dot_general | solution.py:34
  28.4 3.9 %copy.171 = bf16[640,1440]{1,0:T(8,128)(2,1)} copy(bf16[640,1440]{0,1:T(8,128)(2,1)} %convolution_convert_fusion.1) | data formatting | bytes 3686400 | tf_op jit(solution)/shard_map/convert_element_type | solution.py:34
  32.3 4.4 %all-to-all-start.5 = ((bf16[8,80,1440]{2,1,0:T(8,128)(2,1)}), bf16[8,80,1440]{2,1,0:T(8,128)(2,1)}, u32[]{:S(2)}, u32[]{:S(2)}) async-start(bf16[8,80,1440]{2,1,0:T(8,128)(2,1)} %bitcast.117), calls=%async_computation.5 | async-start | bytes 3932160 | tf_op jit(solution)/shard_map/all_to_all | solution.py:35
  37.5 2.6 concatenate.7
  40.1 0.2 fusion.42
  40.3 1.9 convolution_convert_fusion
  42.2 3.8 %copy.154 = bf16[640,1440]{1,0:T(8,128)(2,1)} copy(bf16[640,1440]{0,1:T(8,128)(2,1)} %convolution_convert_fusion) | data formatting | bytes 3686400 | tf_op jit(solution)/shard_map/convert_element_type | solution.py:28
  46.1 14.5 %all-to-all-done.5 = bf16[8,80,1440]{2,1,0:T(8,128)(2,1)} async-done(((bf16[8,80,1440]{2,1,0:T(8,128)(2,1)}), bf16[8,80,1440]{2,1,0:T(8,128)(2,1)}, u32[]{:S(2)}, u32[]{:S(2)}) %all-to-all-start.5) | async-done | bytes 1843232 | tf_op jit(solution)/shard_map/all_to_all | solution.py:35
  60.6 5.8 %all-to-all-start = ((bf16[8,80,1440]{2,1,0:T(8,128)(2,1)}), bf16[8,80,1440]{2,1,0:T(8,128)(2,1)}, u32[]{:S(2)}, u32[]{:S(2)}) async-start(bf16[8,80,1440]{2,1,0:T(8,128)(2,1)} %bitcast.118), calls=%async_computation | async-start | bytes 3932160 | tf_op jit(solution)/shard_map/all_to_all | solution.py:30
  66.4 5.4 %reshape.545 = bf16[8,2,40,4,360]{4,3,2,1,0:T(4,128)(2,1)} reshape(bf16[8,80,1440]{2,1,0:T(8,128)(2,1)} %all-to-all-done.5) | data formatting | bytes 3686400 | tf_op jit(solution)/shard_map/reshape | solution.py:92
  71.8 6.0 %all-gather.3.cloned.1.call-done = bf16[512,1454]{0,1:T(8,128)(2,1)} async-done(((bf16[128,1454]{0,1:T(8,128)(2,1)}), bf16[512,1454]{0,1:T(8,128)(2,1)}) %all-gather.3.cloned.1.call-update) | async-done | bytes 1488912 | tf_op jit(solution)/shard_map/all_gather | solution.py:77
  77.8 2.6 copy.158
  80.4 0.8 slice.52
  81.3 0.6 add_reduce_fusion
  82.6 7.6 %all-to-all-done = bf16[8,80,1440]{2,1,0:T(8,128)(2,1)} async-done(((bf16[8,80,1440]{2,1,0:T(8,128)(2,1)}), bf16[8,80,1440]{2,1,0:T(8,128)(2,1)}, u32[]{:S(2)}, u32[]{:S(2)}) %all-to-all-start) | async-done | bytes 1843232 | tf_op jit(solution)/shard_map/all_to_all | solution.py:30
  90.2 7.0 %fusion = bf16[2,4,360,1440]{3,2,1,0:T(8,128)(2,1)S(1)} fusion(f32[]{:T(128)S(6)} %div.58, bf16[8,2,40,4,360]{4,3,2,1,0:T(4,128)(2,1)} %reshape.545, bf16[8,2,40,1440]{3,2,1,0:T(8,128)(2,1)} %bitcast.8, f32[8,2,40]{2,1,0:T(2,128)S(1)} %reshape.548), kind=kOutput, calls=%fused_computation.4 | convolution fusion | flops 2665267200 | bytes 11983364 | tf_op jit(solution)/shard_map/sjmgf,sjmd->jgfd/dot_general | solution.py:90
  97.2 3.8 %fusion.88 = (bf16[1,4,360,1440]{3,2,1,0:T(8,128)(2,1)}, bf16[1,4,360,1440]{3,2,1,0:T(8,128)(2,1)}) fusion(bf16[2,4,360,1440]{3,2,1,0:T(8,128)(2,1)S(1)} %fusion), kind=kLoop, calls=%fused_computation.154 | loop fusion | bytes 16588800 | tf_op jit(solution)/shard_map/slice | solution.py:100
  101.1 0.2 add.259
  101.4 2.6 copy.159
  104.0 2.1 gather_fusion
  106.1 0.2 broadcast_select_fusion.2
  106.3 1.0 copy-done.2
  107.3 1.1 slice.51
  108.4 1.6 copy.163
  110.0 0.7 fusion.70
  110.8 1.9 fusion.3
  112.7 1.3 convolution_reduce_fusion
  114.1 7.8 %gather_fusion.1 = bf16[1920,1440]{1,0:T(8,128)(2,1)} fusion(bf16[384,1440]{1,0:T(8,128)(2,1)S(1)} %bitcast.113, s32[2048]{0:T(1024)S(1)} %pad_clamp_fusion), kind=kCustom, calls=%fused_computation.1 | custom fusion | bytes 11066880 | tf_op jit(solution)/shard_map/jit(_take)/gather | solution.py:26
  121.9 5.9 %broadcast_select_fusion = bf16[8,240,1440]{2,1,0:T(8,128)(2,1)} fusion(bf16[8,240,1440]{2,1,0:T(8,128)(2,1)} %bitcast.114, pred[8,240]{1,0:T(8,128)(4,1)S(1)} %broadcast_in_dim.49), kind=kLoop, calls=%fused_computation.13 | loop fusion | flops 2764800 | bytes 11061120 | tf_op jit(solution)/shard_map/jit(_take)/select_n | solution.py:26
  127.8 6.0 %all-to-all-start.2 = ((bf16[8,240,1440]{2,1,0:T(8,128)(2,1)}), bf16[8,240,1440]{2,1,0:T(8,128)(2,1)}, u32[]{:S(2)}, u32[]{:S(2)}) async-start(bf16[8,240,1440]{2,1,0:T(8,128)(2,1)} %broadcast_select_fusion), calls=%async_computation.2 | async-start | bytes 11796480 | tf_op jit(solution)/shard_map/all_to_all | solution.py:30
  133.8 0.7 reduce-scatter.3.cloned.1.call-update
  134.5 2.7 fusion.36
  137.2 0.8 copy.156
  138.1 61.7 %all-to-all-done.2 = bf16[8,240,1440]{2,1,0:T(8,128)(2,1)} async-done(((bf16[8,240,1440]{2,1,0:T(8,128)(2,1)}), bf16[8,240,1440]{2,1,0:T(8,128)(2,1)}, u32[]{:S(2)}, u32[]{:S(2)}) %all-to-all-start.2) | async-done | bytes 5529632 | tf_op jit(solution)/shard_map/all_to_all | solution.py:30
  199.8 4.9 %all-to-all-start.1 = ((bf16[8,80,360]{2,1,0:T(8,128)(2,1)}), bf16[8,80,360]{2,1,0:T(8,128)(2,1)S(1)}, u32[]{:S(2)}, u32[]{:S(2)}) async-start(bf16[8,80,360]{2,1,0:T(8,128)(2,1)} %bitcast.14), calls=%async_computation.1 | async-start | bytes 983040 | tf_op jit(solution)/shard_map/all_to_all | solution.py:43
  204.7 5.9 %fusion.22 = bf16[8,3,2,40,360]{4,3,1,0,2:T(8,128)(2,1)S(1)} fusion(bf16[2,360,1440]{2,1,0:T(8,128)(2,1)S(1)} %copy-done, bf16[8,3,2,40,1440]{4,3,2,1,0:T(8,128)(2,1)} %bitcast.24), kind=kOutput, calls=%fused_computation.33 | convolution fusion | flops 1991347200 | bytes 8985600 | tf_op jit(solution)/shard_map/cgjmd,jfd->cgjmf/dot_general | solution.py:42
  210.6 1.3 copy.165
  211.8 0.8 all-to-all-done.1
  212.6 5.6 %all-to-all-start.3 = ((bf16[8,240,360]{2,1,0:T(8,128)(2,1)}), bf16[8,240,360]{2,1,0:T(8,128)(2,1)}, u32[]{:S(2)}, u32[]{:S(2)}) async-start(bf16[8,240,360]{2,1,0:T(8,128)(2,1)} %bitcast.121), calls=%async_computation.3 | async-start | bytes 2949120 | tf_op jit(solution)/shard_map/all_to_all | solution.py:43
  218.3 0.5 fusion.35
  218.9 0.7 slice_convert_fusion.1
  219.7 0.1 reshape.535
  220.2 16.7 %all-to-all-done.3 = bf16[8,240,360]{2,1,0:T(8,128)(2,1)} async-done(((bf16[8,240,360]{2,1,0:T(8,128)(2,1)}), bf16[8,240,360]{2,1,0:T(8,128)(2,1)}, u32[]{:S(2)}, u32[]{:S(2)}) %all-to-all-start.3) | async-done | bytes 1382432 | tf_op jit(solution)/shard_map/all_to_all | solution.py:43
  236.8 4.1 %fusion.9 = bf16[1536,360]{0,1:T(8,128)(2,1)S(1)} fusion(bf16[1920,360]{1,0:T(8,128)(2,1)} %bitcast.29, s32[1536]{0:T(1024)S(1)} %fusion.60), kind=kOutput, calls=%fused_computation.21 | convolution fusion | flops 2126868480 | bytes 2494464 | tf_op jit(solution)/shard_map/dot_general | solution.py:46
  240.9 1.3 pad_maximum_fusion
  242.2 2.6 copy.166
  244.8 3.9 %convert_element_type.159 = bf16[4,128,4,360]{3,2,1,0:T(4,128)(2,1)} reshape(bf16[2048,360]{1,0:T(8,128)(2,1)} %copy.166) | data formatting | bytes 2949120 | tf_op jit(solution)/shard_map/convert_element_type | solution.py:116
  248.7 2.8 copy.167
  251.5 3.3 %gather_fusion.2 = bf16[4,128,4,360]{3,1,2,0:T(8,128)(2,1)} fusion(bf16[4,128,4,360]{3,1,2,0:T(8,128)(2,1)} %copy.167, s32[1024]{0:T(1024)S(1)} %pad_clamp_fusion.1), kind=kCustom, calls=%fused_computation.2 | custom fusion | bytes 2949136 | tf_op jit(solution)/shard_map/jit(_take)/gather | solution.py:118
  254.9 2.8 broadcast_select_fusion.1
  257.7 2.6 copy.168
  260.2 40.0 %all_to_all.40 = bf16[4,128,4,360]{1,3,2,0:T(8,128)(2,1)S(1)} all-to-all(bf16[4,128,4,360]{1,3,2,0:T(8,128)(2,1)} %copy.168), channel_id=1, replica_groups=mesh['grp'=4,'exp'=8] {'grp'}, dimensions={0} | all-to-all | bytes 2949120 | tf_op jit(solution)/shard_map/all_to_all | solution.py:119
  300.3 1.7 fusion.8
  302.0 0.6 multiply_convert_fusion.1
  302.5 4.0 %maximum_convert_fusion = f32[2,360,1440]{2,1,0:T(8,128)} fusion(bf16[1,360,1440]{2,1,0:T(8,128)(2,1)} %bitcast.122, bf16[1,360,1440]{2,1,0:T(8,128)(2,1)} %bitcast.123), kind=kLoop, calls=%fused_computation.22 | loop fusion | flops 2073600 | bytes 6220800 | tf_op jit(solution)/shard_map/convert_element_type | solution.py:101
  (61 shorter events, 2.4 us)
Async XLA Ops:
  7.2 127.3 %copy-start = (bf16[2,360,1440]{2,1,0:T(8,128)(2,1)S(1)}, bf16[2,360,1440]{2,1,0:T(8,128)(2,1)}, u32[]{:S(2)}) copy-start(bf16[2,360,1440]{2,1,0:T(8,128)(2,1)} %param.11) | copy-start | bytes 6220804
  12.6 19.7 %all-to-all-start.6 = ((bf16[8,1,80]{2,1,0:T(2,128)(2,1)}), bf16[8,1,80]{2,1,0:T(2,128)(2,1)S(1)}, u32[]{:S(2)}, u32[]{:S(2)}) async-start(bf16[8,1,80]{2,1,0:T(2,128)(2,1)} %all_to_all.32), calls=%async_computation.6 | async-start | bytes 8192 | tf_op jit(solution)/shard_map/all_to_all | solution.py:31
  32.3 4.5 %copy-start.4 = (s32[128,4]{0,1:T(4,128)S(1)}, s32[128,4]{0,1:T(4,128)}, u32[]{:S(2)}) copy-start(s32[128,4]{0,1:T(4,128)} %param.9) | copy-start | bytes 6148
  32.3 5.2 %copy-start.3 = (bf16[128,1440]{0,1:T(8,128)(2,1)S(1)}, bf16[128,1440]{0,1:T(8,128)(2,1)}, u32[]{:S(2)}) copy-start(bf16[128,1440]{0,1:T(8,128)(2,1)} %param.6) | copy-start | bytes 1105924
  32.3 28.2 %all-to-all-start.5 = ((bf16[8,80,1440]{2,1,0:T(8,128)(2,1)}), bf16[8,80,1440]{2,1,0:T(8,128)(2,1)}, u32[]{:S(2)}, u32[]{:S(2)}) async-start(bf16[8,80,1440]{2,1,0:T(8,128)(2,1)} %bitcast.117), calls=%async_computation.5 | async-start | bytes 3932160 | tf_op jit(solution)/shard_map/all_to_all | solution.py:35
  36.8 41.0 %all-gather.3.cloned.1.call-start = ((), (), s32[]{:S(2)}) async-start(), calls=%async_computation.11 | async-start | bytes 1863680 | tf_op jit(solution)/shard_map/all_gather | solution.py:77
  60.6 29.6 %all-to-all-start = ((bf16[8,80,1440]{2,1,0:T(8,128)(2,1)}), bf16[8,80,1440]{2,1,0:T(8,128)(2,1)}, u32[]{:S(2)}, u32[]{:S(2)}) async-start(bf16[8,80,1440]{2,1,0:T(8,128)(2,1)} %bitcast.118), calls=%async_computation | async-start | bytes 3932160 | tf_op jit(solution)/shard_map/all_to_all | solution.py:30
  66.3 236.2 %reduce-scatter.5.cloned.1.call-start = ((), (), s32[]{:S(2)}) async-start(), calls=%async_computation.10 | async-start | bytes 5529600 | tf_op jit(solution)/shard_map/reduce_scatter | solution.py:100
  106.3 1.0 copy-start.2
  127.8 72.0 %all-to-all-start.2 = ((bf16[8,240,1440]{2,1,0:T(8,128)(2,1)}), bf16[8,240,1440]{2,1,0:T(8,128)(2,1)}, u32[]{:S(2)}, u32[]{:S(2)}) async-start(bf16[8,240,1440]{2,1,0:T(8,128)(2,1)} %broadcast_select_fusion), calls=%async_computation.2 | async-start | bytes 11796480 | tf_op jit(solution)/shard_map/all_to_all | solution.py:30
  133.8 168.8 %reduce-scatter.3.cloned.1.call-start = ((), (), s32[]{:S(2)}) async-start(), calls=%async_computation.9 | async-start | bytes 5529600 | tf_op jit(solution)/shard_map/reduce_scatter | solution.py:100
  199.8 12.9 %all-to-all-start.1 = ((bf16[8,80,360]{2,1,0:T(8,128)(2,1)}), bf16[8,80,360]{2,1,0:T(8,128)(2,1)S(1)}, u32[]{:S(2)}, u32[]{:S(2)}) async-start(bf16[8,80,360]{2,1,0:T(8,128)(2,1)} %bitcast.14), calls=%async_computation.1 | async-start | bytes 983040 | tf_op jit(solution)/shard_map/all_to_all | solution.py:43
  212.6 24.2 %all-to-all-start.3 = ((bf16[8,240,360]{2,1,0:T(8,128)(2,1)}), bf16[8,240,360]{2,1,0:T(8,128)(2,1)}, u32[]{:S(2)}, u32[]{:S(2)}) async-start(bf16[8,240,360]{2,1,0:T(8,128)(2,1)} %bitcast.121), calls=%async_computation.3 | async-start | bytes 2949120 | tf_op jit(solution)/shard_map/all_to_all | solution.py:43
  260.2 40.1 %copy-start.1 = (bf16[128,4,1440]{0,2,1:T(8,128)(2,1)S(1)}, bf16[128,4,1440]{0,2,1:T(8,128)(2,1)}, u32[]{:S(2)}) copy-start(bf16[128,4,1440]{0,2,1:T(8,128)(2,1)} %param.7) | copy-start | bytes 4423684
Sparse Core Ops, SparseCore 0:
  40.2 37.5 all-gather.2
  101.2 80.8 reduce-scatter.4
  185.0 80.9 reduce-scatter.2

commit v4 on v2

--- a/solution.py
+++ b/solution.py
@@ -109,8 +109,15 @@
     proj_rel = jnp.concatenate(
         [proj_home(pick_a, dy_a, w_down, 1, most), proj_home(pick_b, dy_b, w_down, n_b, most)]
     ).astype(jnp.bfloat16).reshape(n_grp, tok, top, f_loc)
-    back = (jnp.arange(n_grp, dtype=jnp.int32) - me) % n_grp
-    proj_slot = jnp.take(proj_rel, back, axis=0)
+    proj_slot = jnp.stack(
+        [
+            sum(
+                jnp.where((a - me) % n_grp == i, proj_rel[i], jnp.zeros((), proj_rel.dtype))
+                for i in range(n_grp)
+            )
+            for a in range(n_grp)
+        ]
+    )
     proj_got = lax.all_to_all(proj_slot, "grp", split_axis=0, concat_axis=0, tiled=True)
     proj = jnp.transpose(proj_got, (1, 2, 0, 3)).reshape(tok, top, ffw).astype(jnp.float32)
 

time: 314 us -> 319 us (1.016)
  waiting for transfers between devices: 108 us -> 112 us
  local copies, waits for them, and re-layouts: 67.6 us -> 64.3 us
    add x0 -> x8, local copies, waits for them, and re-layouts: none -> 8.4 us  [body(): sum((jnp.where((a - me) % n_grp == i, proj_rel[i], jnp.zeros((), proj_rel...]
    convert_element_type x2 -> x0, local copies, waits for them, and re-layouts: 6.8 us -> none  [body(): proj_rel = jnp.concatenate([proj_home(pick_a, dy_a, w_down, 1, most), pro...]
    another operation x4 -> x5, local copies, waits for them, and re-layouts: 0.19 us -> 3.84 us  [the longest x1 3.65 us: body(): jnp.stack([sum((jnp.where((a - me) % n_grp == i, proj_rel[i], jnp.zeros((...]
    all_to_all x2, waiting for transfers between devices: 69.3 us -> 72.9 us  [dispatch(): lax.all_to_all(dy_buf.reshape(n_exp, per_dest, -1), 'exp', 0, 0, tiled=True)]
    gather x1 -> x0, local copies, waits for them, and re-layouts: 3.33 us -> none  [body(): proj_slot = jnp.take(proj_rel, back, axis=0)]
    another operation x2 -> x3, other arithmetic: 1.18 us -> 4.51 us  [the longest x1 3.32 us: body(): jnp.stack([sum((jnp.where((a - me) % n_grp == i, proj_rel[i], jnp.zeros((...]
where the time goes in v4:
time: 319 us; the launch traced here: 317 us
  waiting for transfers between devices  112 us (35%)
  local copies, waits for them, and re-layouts  64.3 us (20%)
  blocking collectives  40 us (13%)
  matrix products  35 us (11%)
  starting transfers between devices  31.9 us (10%)
  other arithmetic  18.4 us (6%)
  between operations  15.4 us (5%)
    all_to_all x2, waiting for transfers between devices, dispatch(): lax.all_to_all(dy_buf.reshape(n_exp, per_dest, -1), 'exp', 0, 0, tiled=True)  72.9 us
    all_to_all x1, blocking collectives, body(): lax.all_to_all(proj_slot, 'grp', split_axis=0, concat_axis=0, tiled=True)  40 us
    all_to_all x2, waiting for transfers between devices, proj_home(): lax.all_to_all(proj.astype(jnp.bfloat16).reshape(n_exp, n * exp_dev * mos...  17.7 us
    all_to_all x1, waiting for transfers between devices, dispatch(): lax.all_to_all(hid_buf.reshape(n_exp, per_dest, -1), 'exp', 0, 0, tiled=T...  14.5 us
    all_to_all x2, starting transfers between devices, dispatch(): lax.all_to_all(dy_buf.reshape(n_exp, per_dest, -1), 'exp', 0, 0, tiled=True)  11.9 us
    all_to_all x2, starting transfers between devices, proj_home(): lax.all_to_all(proj.astype(jnp.bfloat16).reshape(n_exp, n * exp_dev * mos...  11.3 us
    dot_general x2, matrix products, proj_home(): jnp.einsum('cgjmd,jfd->cgjmf', dy_r, w_down, preferred_element_type=jnp.f...  8.6 us
    reshape x1, local copies, waits for them, and re-layouts, dispatch(): dy_buf.reshape(n_exp, per_dest, -1)  8.4 us
  transfers between devices with their start and end apart: 9, of which 6 were waited for; matrix products, arithmetic and copies ran while one was open for 31% of the time, Pallas kernels for 0%

profile of v4, /device:TPU:2, one launch (start us, length us, event | category | flops | bytes accessed | tf_op | source)
XLA Modules:
  0.0 316.8 jit_solution(7157325064513841677)
XLA Ops:
  7.2 0.9 copy.158
  8.3 1.2 reduce-window.6
  9.4 0.2 slice_reduce_fusion
  10.3 0.7 fusion.83
  11.6 0.3 fusion.41
  11.9 0.7 all_to_all.32
  12.6 4.3 %all-to-all-start.6 = ((bf16[8,1,80]{2,1,0:T(2,128)(2,1)}), bf16[8,1,80]{2,1,0:T(2,128)(2,1)S(1)}, u32[]{:S(2)}, u32[]{:S(2)}) async-start(bf16[8,1,80]{2,1,0:T(2,128)(2,1)} %all_to_all.32), calls=%async_computation.6 | async-start | bytes 8192 | tf_op jit(solution)/shard_map/all_to_all | solution.py:26
  16.9 3.8 %copy.189 = bf16[128,4,1440]{2,1,0:T(4,128)(2,1)} copy(bf16[128,4,1440]{0,2,1:T(8,128)(2,1)} %param.7) | data formatting | bytes 2949120 | tf_op args[1]
  20.7 3.7 %reshape.743 = bf16[512,1440]{1,0:T(8,128)(2,1)} reshape(bf16[128,4,1440]{2,1,0:T(4,128)(2,1)} %copy.189) | data formatting | bytes 2949120 | tf_op jit(solution)/shard_map/reshape | solution.py:79
  24.4 4.0 %convolution_convert_fusion.2 = bf16[640,1440]{0,1:T(8,128)(2,1)} fusion(bf16[512,1440]{1,0:T(8,128)(2,1)} %reshape.743, s32[512]{0:T(512)S(1)} %fusion.77), kind=kOutput, calls=%fused_computation.14 | convolution fusion | flops 944967680 | bytes 3319808 | tf_op jit(solution)/shard_map/dot_general | solution.py:29
  28.4 3.9 %copy.190 = bf16[640,1440]{1,0:T(8,128)(2,1)} copy(bf16[640,1440]{0,1:T(8,128)(2,1)} %convolution_convert_fusion.2) | data formatting | bytes 3686400 | tf_op jit(solution)/shard_map/convert_element_type | solution.py:29
  32.3 4.4 %all-to-all-start.5 = ((bf16[8,80,1440]{2,1,0:T(8,128)(2,1)}), bf16[8,80,1440]{2,1,0:T(8,128)(2,1)}, u32[]{:S(2)}, u32[]{:S(2)}) async-start(bf16[8,80,1440]{2,1,0:T(8,128)(2,1)} %bitcast.115), calls=%async_computation.5 | async-start | bytes 3932160 | tf_op jit(solution)/shard_map/all_to_all | solution.py:30
  37.5 2.6 concatenate.5
  40.1 0.2 fusion.42
  40.3 1.9 convolution_convert_fusion.1
  42.2 3.8 %copy.170 = bf16[640,1440]{1,0:T(8,128)(2,1)} copy(bf16[640,1440]{0,1:T(8,128)(2,1)} %convolution_convert_fusion.1) | data formatting | bytes 3686400 | tf_op jit(solution)/shard_map/convert_element_type | solution.py:23
  46.1 14.5 %all-to-all-done.5 = bf16[8,80,1440]{2,1,0:T(8,128)(2,1)} async-done(((bf16[8,80,1440]{2,1,0:T(8,128)(2,1)}), bf16[8,80,1440]{2,1,0:T(8,128)(2,1)}, u32[]{:S(2)}, u32[]{:S(2)}) %all-to-all-start.5) | async-done | bytes 1843232 | tf_op jit(solution)/shard_map/all_to_all | solution.py:30
  60.6 5.8 %all-to-all-start = ((bf16[8,80,1440]{2,1,0:T(8,128)(2,1)}), bf16[8,80,1440]{2,1,0:T(8,128)(2,1)}, u32[]{:S(2)}, u32[]{:S(2)}) async-start(bf16[8,80,1440]{2,1,0:T(8,128)(2,1)} %bitcast.116), calls=%async_computation | async-start | bytes 3932160 | tf_op jit(solution)/shard_map/all_to_all | solution.py:25
  66.4 5.4 %reshape.745 = bf16[8,2,40,4,360]{4,3,2,1,0:T(4,128)(2,1)} reshape(bf16[8,80,1440]{2,1,0:T(8,128)(2,1)} %all-to-all-done.5) | data formatting | bytes 3686400 | tf_op jit(solution)/shard_map/reshape | solution.py:87
  71.8 6.0 %all-gather.3.cloned.1.call-done = bf16[512,1454]{0,1:T(8,128)(2,1)} async-done(((bf16[128,1454]{0,1:T(8,128)(2,1)}), bf16[512,1454]{0,1:T(8,128)(2,1)}) %all-gather.3.cloned.1.call-update) | async-done | bytes 1488912 | tf_op jit(solution)/shard_map/all_gather | solution.py:72
  77.8 2.6 copy.174
  80.4 0.8 slice.86
  81.3 0.6 add_reduce_fusion
  82.6 7.6 %all-to-all-done = bf16[8,80,1440]{2,1,0:T(8,128)(2,1)} async-done(((bf16[8,80,1440]{2,1,0:T(8,128)(2,1)}), bf16[8,80,1440]{2,1,0:T(8,128)(2,1)}, u32[]{:S(2)}, u32[]{:S(2)}) %all-to-all-start) | async-done | bytes 1843232 | tf_op jit(solution)/shard_map/all_to_all | solution.py:25
  90.2 7.0 %fusion = bf16[2,4,360,1440]{3,2,1,0:T(8,128)(2,1)S(1)} fusion(f32[]{:T(128)S(6)} %div.58, bf16[8,2,40,4,360]{4,3,2,1,0:T(4,128)(2,1)} %reshape.745, bf16[8,2,40,1440]{3,2,1,0:T(8,128)(2,1)} %bitcast.8, f32[8,2,40]{2,1,0:T(2,128)S(1)} %reshape.748), kind=kOutput, calls=%fused_computation.2 | convolution fusion | flops 2665267200 | bytes 11983364 | tf_op jit(solution)/shard_map/sjmgf,sjmd->jgfd/dot_general | solution.py:85
  97.2 3.8 %fusion.84 = (bf16[1,4,360,1440]{3,2,1,0:T(8,128)(2,1)}, bf16[1,4,360,1440]{3,2,1,0:T(8,128)(2,1)}) fusion(bf16[2,4,360,1440]{3,2,1,0:T(8,128)(2,1)S(1)} %fusion), kind=kLoop, calls=%fused_computation.137 | loop fusion | bytes 16588800 | tf_op jit(solution)/shard_map/slice | solution.py:95
  101.1 0.2 add.382
  101.4 2.6 copy.175
  104.0 2.1 gather_fusion
  106.1 0.2 broadcast_select_fusion
  106.3 1.0 copy-done.2
  107.4 1.7 copy.179
  109.1 0.7 fusion.70
  109.8 1.9 fusion.3
  111.7 6.4 %convolution_convert_fusion = bf16[1920,1440]{0,1:T(8,128)(2,1)} fusion(bf16[1920,384]{1,0:T(8,128)(2,1)S(1)} %fusion.3, bf16[384,1440]{1,0:T(8,128)(2,1)} %bitcast.120), kind=kOutput, calls=%fused_computation.7 | convolution fusion | flops 2126131200 | bytes 8110080 | tf_op jit(solution)/shard_map/dot_general | solution.py:23
  118.1 8.4 %copy.200 = bf16[1920,1440]{1,0:T(8,128)(2,1)} copy(bf16[1920,1440]{0,1:T(8,128)(2,1)} %convolution_convert_fusion) | data formatting | bytes 11059200 | tf_op jit(solution)/shard_map/reshape | solution.py:25
  126.5 6.1 %all-to-all-start.2 = ((bf16[8,240,1440]{2,1,0:T(8,128)(2,1)}), bf16[8,240,1440]{2,1,0:T(8,128)(2,1)}, u32[]{:S(2)}, u32[]{:S(2)}) async-start(bf16[8,240,1440]{2,1,0:T(8,128)(2,1)} %bitcast.112), calls=%async_computation.2 | async-start | bytes 11796480 | tf_op jit(solution)/shard_map/all_to_all | solution.py:25
  132.7 0.7 reduce-scatter.3.cloned.1.call-update
  133.4 65.3 %all-to-all-done.2 = bf16[8,240,1440]{2,1,0:T(8,128)(2,1)} async-done(((bf16[8,240,1440]{2,1,0:T(8,128)(2,1)}), bf16[8,240,1440]{2,1,0:T(8,128)(2,1)}, u32[]{:S(2)}, u32[]{:S(2)}) %all-to-all-start.2) | async-done | bytes 5529632 | tf_op jit(solution)/shard_map/all_to_all | solution.py:25
  198.6 5.9 %fusion.22 = bf16[8,3,2,40,360]{4,3,1,0,2:T(8,128)(2,1)S(1)} fusion(bf16[2,360,1440]{2,1,0:T(8,128)(2,1)S(1)} %copy-done, bf16[8,3,2,40,1440]{4,3,2,1,0:T(8,128)(2,1)} %bitcast.24), kind=kOutput, calls=%fused_computation.30 | convolution fusion | flops 1991347200 | bytes 8985600 | tf_op jit(solution)/shard_map/cgjmd,jfd->cgjmf/dot_general | solution.py:37
  204.5 1.3 copy.182
  205.8 5.8 %all-to-all-start.3 = ((bf16[8,240,360]{2,1,0:T(8,128)(2,1)}), bf16[8,240,360]{2,1,0:T(8,128)(2,1)}, u32[]{:S(2)}, u32[]{:S(2)}) async-start(bf16[8,240,360]{2,1,0:T(8,128)(2,1)} %bitcast.119), calls=%async_computation.3 | async-start | bytes 2949120 | tf_op jit(solution)/shard_map/all_to_all | solution.py:38
  211.6 2.7 fusion.36
  214.3 0.8 copy.172
  215.1 0.7 slice_convert_fusion.1
  216.0 0.1 reshape.734
  216.4 13.7 %all-to-all-done.3 = bf16[8,240,360]{2,1,0:T(8,128)(2,1)} async-done(((bf16[8,240,360]{2,1,0:T(8,128)(2,1)}), bf16[8,240,360]{2,1,0:T(8,128)(2,1)}, u32[]{:S(2)}, u32[]{:S(2)}) %all-to-all-start.3) | async-done | bytes 1382432 | tf_op jit(solution)/shard_map/all_to_all | solution.py:38
  230.1 5.5 %all-to-all-start.1 = ((bf16[8,80,360]{2,1,0:T(8,128)(2,1)}), bf16[8,80,360]{2,1,0:T(8,128)(2,1)}, u32[]{:S(2)}, u32[]{:S(2)}) async-start(bf16[8,80,360]{2,1,0:T(8,128)(2,1)} %bitcast.14), calls=%async_computation.1 | async-start | bytes 983040 | tf_op jit(solution)/shard_map/all_to_all | solution.py:38
  235.7 4.1 %fusion.9 = bf16[1536,360]{0,1:T(8,128)(2,1)S(1)} fusion(bf16[1920,360]{1,0:T(8,128)(2,1)} %bitcast.29, s32[1536]{0:T(1024)S(1)} %fusion.60), kind=kOutput, calls=%fused_computation.19 | convolution fusion | flops 2126868480 | bytes 2494464 | tf_op jit(solution)/shard_map/dot_general | solution.py:41
  239.8 4.0 %all-to-all-done.1 = bf16[8,80,360]{2,1,0:T(8,128)(2,1)} async-done(((bf16[8,80,360]{2,1,0:T(8,128)(2,1)}), bf16[8,80,360]{2,1,0:T(8,128)(2,1)}, u32[]{:S(2)}, u32[]{:S(2)}) %all-to-all-start.1) | async-done | bytes 460832 | tf_op jit(solution)/shard_map/all_to_all | solution.py:38
  243.7 2.7 select_add_fusion.3
  246.4 1.2 copy.183
  247.7 2.3 select_add_fusion.2
  250.0 0.2 copy.184
  250.3 1.9 copy.186
  252.3 1.1 add.405
  253.4 1.9 copy.185
  255.3 1.8 add.400
  257.1 3.3 %pad_maximum_fusion = bf16[4,128,4,360]{3,2,1,0:T(4,128)(2,1)} fusion(bf16[1,128,4,360]{3,2,1,0:T(4,128)(2,1)S(1)} %add.405, bf16[1,128,4,360]{3,2,1,0:T(4,128)(2,1)} %add.400, bf16[1,128,4,360]{3,2,1,0:T(4,128)(2,1)S(1)} %add.395, bf16[1,128,4,360]{3,2,1,0:T(4,128)(2,1)S(1)} %add.390), kind=kLoop, calls=%fused_computation.29 | loop fusion | flops 2211840 | bytes 2949120 | tf_op jit(solution)/shard_map/stack | solution.py:112
  260.4 3.7 %copy.187 = bf16[4,128,4,360]{1,3,2,0:T(8,128)(2,1)} copy(bf16[4,128,4,360]{3,2,1,0:T(4,128)(2,1)} %pad_maximum_fusion) | data formatting | bytes 2949120 | tf_op jit(solution)/shard_map/stack | solution.py:112
  264.1 40.0 %all_to_all.40 = bf16[4,128,4,360]{1,3,2,0:T(8,128)(2,1)S(1)} all-to-all(bf16[4,128,4,360]{1,3,2,0:T(8,128)(2,1)} %copy.187), channel_id=1, replica_groups=mesh['grp'=4,'exp'=8] {'grp'}, dimensions={0} | all-to-all | bytes 2949120 | tf_op jit(solution)/shard_map/all_to_all | solution.py:121
  304.1 1.7 fusion.8
  305.8 0.6 multiply_convert_fusion.1
  306.3 4.0 %maximum_convert_fusion = f32[2,360,1440]{2,1,0:T(8,128)} fusion(bf16[1,360,1440]{2,1,0:T(8,128)(2,1)} %bitcast.121, bf16[1,360,1440]{2,1,0:T(8,128)(2,1)} %bitcast.122), kind=kLoop, calls=%fused_computation.20 | loop fusion | flops 2073600 | bytes 6220800 | tf_op jit(solution)/shard_map/convert_element_type | solution.py:96
  (59 shorter events, 2.6 us)
Async XLA Ops:
  7.2 191.5 %copy-start = (bf16[2,360,1440]{2,1,0:T(8,128)(2,1)S(1)}, bf16[2,360,1440]{2,1,0:T(8,128)(2,1)}, u32[]{:S(2)}) copy-start(bf16[2,360,1440]{2,1,0:T(8,128)(2,1)} %param.11) | copy-start | bytes 6220804
  12.6 19.7 %all-to-all-start.6 = ((bf16[8,1,80]{2,1,0:T(2,128)(2,1)}), bf16[8,1,80]{2,1,0:T(2,128)(2,1)S(1)}, u32[]{:S(2)}, u32[]{:S(2)}) async-start(bf16[8,1,80]{2,1,0:T(2,128)(2,1)} %all_to_all.32), calls=%async_computation.6 | async-start | bytes 8192 | tf_op jit(solution)/shard_map/all_to_all | solution.py:26
  32.3 4.5 %copy-start.5 = (s32[128,4]{0,1:T(4,128)S(1)}, s32[128,4]{0,1:T(4,128)}, u32[]{:S(2)}) copy-start(s32[128,4]{0,1:T(4,128)} %param.9) | copy-start | bytes 6148
  32.3 5.2 %copy-start.3 = (bf16[128,1440]{0,1:T(8,128)(2,1)S(1)}, bf16[128,1440]{0,1:T(8,128)(2,1)}, u32[]{:S(2)}) copy-start(bf16[128,1440]{0,1:T(8,128)(2,1)} %param.6) | copy-start | bytes 1105924
  32.3 28.2 %all-to-all-start.5 = ((bf16[8,80,1440]{2,1,0:T(8,128)(2,1)}), bf16[8,80,1440]{2,1,0:T(8,128)(2,1)}, u32[]{:S(2)}, u32[]{:S(2)}) async-start(bf16[8,80,1440]{2,1,0:T(8,128)(2,1)} %bitcast.115), calls=%async_computation.5 | async-start | bytes 3932160 | tf_op jit(solution)/shard_map/all_to_all | solution.py:30
  36.8 41.0 %all-gather.3.cloned.1.call-start = ((), (), s32[]{:S(2)}) async-start(), calls=%async_computation.11 | async-start | bytes 1863680 | tf_op jit(solution)/shard_map/all_gather | solution.py:72
  60.6 29.6 %all-to-all-start = ((bf16[8,80,1440]{2,1,0:T(8,128)(2,1)}), bf16[8,80,1440]{2,1,0:T(8,128)(2,1)}, u32[]{:S(2)}, u32[]{:S(2)}) async-start(bf16[8,80,1440]{2,1,0:T(8,128)(2,1)} %bitcast.116), calls=%async_computation | async-start | bytes 3932160 | tf_op jit(solution)/shard_map/all_to_all | solution.py:25
  66.3 240.0 %reduce-scatter.5.cloned.1.call-start = ((), (), s32[]{:S(2)}) async-start(), calls=%async_computation.10 | async-start | bytes 5529600 | tf_op jit(solution)/shard_map/reduce_scatter | solution.py:95
  106.3 1.0 copy-start.2
  126.5 72.1 %all-to-all-start.2 = ((bf16[8,240,1440]{2,1,0:T(8,128)(2,1)}), bf16[8,240,1440]{2,1,0:T(8,128)(2,1)}, u32[]{:S(2)}, u32[]{:S(2)}) async-start(bf16[8,240,1440]{2,1,0:T(8,128)(2,1)} %bitcast.112), calls=%async_computation.2 | async-start | bytes 11796480 | tf_op jit(solution)/shard_map/all_to_all | solution.py:25
  132.6 173.7 %reduce-scatter.3.cloned.1.call-start = ((), (), s32[]{:S(2)}) async-start(), calls=%async_computation.9 | async-start | bytes 5529600 | tf_op jit(solution)/shard_map/reduce_scatter | solution.py:95
  205.8 24.4 %all-to-all-start.3 = ((bf16[8,240,360]{2,1,0:T(8,128)(2,1)}), bf16[8,240,360]{2,1,0:T(8,128)(2,1)}, u32[]{:S(2)}, u32[]{:S(2)}) async-start(bf16[8,240,360]{2,1,0:T(8,128)(2,1)} %bitcast.119), calls=%async_computation.3 | async-start | bytes 2949120 | tf_op jit(solution)/shard_map/all_to_all | solution.py:38
  230.1 13.6 %all-to-all-start.1 = ((bf16[8,80,360]{2,1,0:T(8,128)(2,1)}), bf16[8,80,360]{2,1,0:T(8,128)(2,1)}, u32[]{:S(2)}, u32[]{:S(2)}) async-start(bf16[8,80,360]{2,1,0:T(8,128)(2,1)} %bitcast.14), calls=%async_computation.1 | async-start | bytes 983040 | tf_op jit(solution)/shard_map/all_to_all | solution.py:38
  239.7 6.6 %copy-start.4 = (bf16[1536,360]{0,1:T(8,128)(2,1)}, bf16[1536,360]{0,1:T(8,128)(2,1)S(1)}, u32[]{:S(2)}) copy-start(bf16[1536,360]{0,1:T(8,128)(2,1)S(1)} %fusion.9) | copy-start | bytes 3317764
  264.1 40.0 %copy-start.1 = (bf16[128,4,1440]{0,2,1:T(8,128)(2,1)S(1)}, bf16[128,4,1440]{0,2,1:T(8,128)(2,1)}, u32[]{:S(2)}) copy-start(bf16[128,4,1440]{0,2,1:T(8,128)(2,1)} %param.7) | copy-start | bytes 4423684
Sparse Core Ops, SparseCore 0:
  40.2 37.5 all-gather.2
  101.2 80.8 reduce-scatter.4
  185.0 80.9 reduce-scatter.2
